TPU v7x, 32 devices: a whole 2x2x4 slice. The times are simulated.
32 devices in a mesh: grp: 4 (over z), node: 8 (over y, x, core).
Axes of the slice: x: 2, y: 2, z: 4, core: 2. Of those that a mesh axis runs over, the one named last changes fastest.
Arguments:
- params: bfloat16 [4, 14336, 4096], P('grp', 'node'), may hold values from -6 to 6
- momentum: bfloat16 [4, 14336, 4096], P('grp', 'node'), may hold values from -0.125 to 0.125
- hidden: bfloat16 [4, 1024, 14336], P('grp', 'node'), may hold values from -6 to 6
- cotangent: bfloat16 [4, 1024, 4096], P('grp', 'node'), may hold values from -6 to 6
- push_weight: float32 [4], P('grp'), may hold values from 0.5 to 2
- offsets: int32 [64], replicated, may hold values from 1 to 3
- step: int32 [1], replicated, may hold values from 0 to 63
Outputs:
- mixed: bfloat16 [4, 14336, 4096], P('grp', 'node')
- new_weight: float32 [4], P('grp')
All inputs are finite; a program needn't handle non-finite values.
Results may differ from a plain program's by a relative error of at most 0.005.
Values may be sent and summed in bfloat16 or wider, within the bound.
No kernel may reach another device: no remote copies, remote signals or barrier semaphores. Data moves between devices by JAX's collectives and lax.ppermute only.
A program may use at most 192 MiB of HBM per device.

v0:
```python
from functools import partial

import jax
import jax.numpy as jnp
from jax import lax
from jax.sharding import PartitionSpec as P

base_rate = 40.0
moment_decay = 0.9
keep_share = 0.5
back_share = 0.3
front_share = 0.2
tokens_axis = (((0,), (0,)), ((), ()))


def shortened(array):
    return jax.tree.map(lambda a: a.astype(jnp.bfloat16) if a.dtype == jnp.float32 else a, array)


def shifted(value, axis, steps):
    count = lax.axis_size(axis)
    pairs = [(source, (source + steps) % count) for source in range(count)]
    return lax.ppermute(value, axis, pairs)


def neighbours(halfway, weight, amount, groups):
    behind = jax.tree.map(
        lambda part, own: part.astype(own.dtype),
        shifted(shortened(halfway), "grp", amount),
        halfway,
    )
    ahead = jax.tree.map(
        lambda part, own: part.astype(own.dtype),
        shifted(shortened(halfway), "grp", groups - amount),
        halfway,
    )
    weight_behind = shifted(weight, "grp", amount)
    weight_ahead = shifted(weight, "grp", groups - amount)
    peers = back_share * behind.astype(jnp.float32) + front_share * ahead.astype(jnp.float32)
    peer_weight = back_share * weight_behind + front_share * weight_ahead
    return (peers, peer_weight)


def per_device(params, momentum, hidden, cotangent, push_weight, offsets, step):
    groups = lax.axis_size("grp")
    nodes = lax.axis_size("node")
    acts = hidden[0]
    cots = cotangent[0]
    tok_local = acts.shape[0]
    tok_group = tok_local * nodes
    columns = lax.all_to_all(acts, "node", split_axis=1, concat_axis=0, tiled=True)
    grad = lax.dot_general(
        columns,
        lax.all_gather(cots, "node", axis=0, tiled=True),
        tokens_axis,
        preferred_element_type=jnp.float32,
    )
    grad = grad / tok_group
    position = step[0]
    offset = offsets[position]
    rate = base_rate * (1.0 - 0.5 * position.astype(jnp.float32) / offsets.shape[0])
    renewed = moment_decay * momentum[0].astype(jnp.float32) + grad
    halfway = (params[0].astype(jnp.float32) - rate * renewed).astype(jnp.bfloat16)
    branches = [partial(neighbours, amount=amount, groups=groups) for amount in range(1, groups)]
    peers, peer_weight = lax.switch(offset - 1, branches, halfway, push_weight)
    mixed = (keep_share * halfway.astype(jnp.float32) + peers).astype(jnp.bfloat16)
    new_weight = keep_share * push_weight + peer_weight
    return (mixed[None], new_weight)


def solution(mesh):
    in_specs = (
        P("grp", "node", None),
        P("grp", "node", None),
        P("grp", "node", None),
        P("grp", "node", None),
        P("grp"),
        P(),
        P(),
    )
    out_specs = (P("grp", "node", None), P("grp"))
    return jax.shard_map(
        per_device, mesh=mesh, in_specs=in_specs, out_specs=out_specs, check_vma=False
    )
```

profile of v0, /device:TPU:0, one launch (start us, length us, event | category | flops | bytes accessed | tf_op | source)
XLA Modules:
  0.0 811.3 jit_solution(12599189888778378843)
XLA Ops:
  7.2 0.0 all-gather.3.cloned.1.call-start
  7.2 0.7 all-gather.3.cloned.1.call-update
  7.9 6.1 copy.9
  13.9 5.2 all-to-all-start
  20.4 1.2 dynamic_slice.3
  22.4 51.6 %all-to-all-done = bf16[128,8,1792]{0,2,1:T(8,128)(2,1)} async-done(((bf16[128,8,1792]{0,2,1:T(8,128)(2,1)}), bf16[128,8,1792]{0,2,1:T(8,128)(2,1)}, u32[]{:S(2)}, u32[]{:S(2)}) %all-to-all-start) | async-done | bytes 3670048 | tf_op jit(solution)/shard_map/all_to_all | solution.py:51
  74.0 5.9 copy.10
  79.9 18.4 %all-gather.3.cloned.1.call-done = bf16[1,1024,4096]{2,1,0:T(8,128)(2,1)} async-done(((bf16[1,128,4096]{2,1,0:T(8,128)(2,1)}), bf16[1,1024,4096]{2,1,0:T(8,128)(2,1)}) %all-gather.3.cloned.1.call-update) | async-done | bytes 8388624 | tf_op jit(solution)/shard_map/all_gather | solution.py:54
  98.3 26.8 %fusion = bf16[1792,4096]{1,0:T(8,128)(2,1)S(1)} fusion(bf16[1,1792,4096]{2,1,0:T(8,128)(2,1)} %param.11, bf16[1024,1792]{1,0:T(8,128)(2,1)} %bitcast.25, bf16[1,1792,4096]{2,1,0:T(8,128)(2,1)} %param.10, f32[]{:T(128)S(6)} %mul_shard_map.3, bf16[1,1024,4096]{2,1,0:T(8,128)(2,1)} %all-gather.3.cloned.1.call-done), kind=kOutput, calls=%fused_computation.4 | convolution fusion | flops 15091105792 | bytes 56098820 | tf_op jit(solution)/shard_map/dot_general | solution.py:52
  125.1 0.0 copy-start
  125.1 5.5 copy-done
  130.6 652.4 %conditional.1 = (f32[1792,4096]{1,0:T(8,128)}, f32[1]{0:T(128)}) conditional(s32[]{:T(128)} %bitcast.7, (bf16[1792,4096]{1,0:T(8,128)(2,1)S(1)}, f32[1]{0:T(128)}) %tuple.20, (bf16[1792,4096]{1,0:T(8,128)(2,1)S(1)}, f32[1]{0:T(128)}) %tuple.20, (bf16[1792,4096]{1,0:T(8,128)(2,1)S(1)}, f32[1]{0:T(128)}) %tuple.20), branch_computations={%region_0.0_spmd, %region_1.0_spmd, %region_2.0_spmd} | conditional | flops 36700160 | bytes 176161008 | solution.py:65
  130.6 4.1 collective-permute-start.6
  134.7 0.0 collective-permute-start.7
  134.7 3.8 collective-permute-start.8
  138.5 0.0 collective-permute-start.9
  138.5 625.8 %collective-permute-done.8 = f32[1]{0:T(128)} collective-permute-done((f32[1]{0:T(128)}, f32[1]{0:T(128)}, u32[]{:S(2)}, u32[]{:S(2)}) %collective-permute-start.8) | collective-permute-done | bytes 36 | tf_op jit(solution)/shard_map/cond/branch_2_fun/ppermute | solution.py:23
  764.9 0.5 collective-permute-done.9
  766.0 0.0 collective-permute-done.6
  766.1 0.0 collective-permute-done.7
  766.1 17.0 %multiply_add_fusion.1 = f32[1792,4096]{1,0:T(8,128)} fusion(bf16[1792,4096]{1,0:T(8,128)(2,1)} %collective-permute-done.7, bf16[1792,4096]{1,0:T(8,128)(2,1)S(1)} %collective-permute-done.6), kind=kLoop, calls=%fused_computation.2 | loop fusion | flops 36700160 | bytes 58720256 | tf_op jit(solution)/shard_map/cond/branch_2_fun/add | solution.py:39
  783.0 20.3 %fusion.2 = bf16[1,1792,4096]{2,1,0:T(8,128)(2,1)} fusion(f32[1792,4096]{1,0:T(8,128)} %get-tuple-element.22, bf16[1792,4096]{1,0:T(8,128)(2,1)} %copy-done), kind=kLoop, calls=%fused_computation.8 | loop fusion | flops 29360128 | bytes 58720256 | tf_op jit(solution)/shard_map/broadcast_in_dim | solution.py:68
Async XLA Ops:
  7.2 91.1 %all-gather.3.cloned.1.call-start = ((), (), s32[]{:S(2)}) async-start(), calls=%async_computation.1 | async-start | bytes 9437184 | tf_op jit(solution)/shard_map/all_gather | solution.py:54
  13.9 60.0 %all-to-all-start = ((bf16[128,8,1792]{0,2,1:T(8,128)(2,1)}), bf16[128,8,1792]{0,2,1:T(8,128)(2,1)}, u32[]{:S(2)}, u32[]{:S(2)}) async-start(bf16[128,8,1792]{0,2,1:T(8,128)(2,1)} %bitcast.24), calls=%async_computation | async-start | bytes 7340032 | tf_op jit(solution)/shard_map/all_to_all | solution.py:51
  125.1 5.5 copy-start
  130.6 635.4 %collective-permute-start.6 = (bf16[1792,4096]{1,0:T(8,128)(2,1)S(1)}, bf16[1792,4096]{1,0:T(8,128)(2,1)S(1)}, u32[]{:S(2)}, u32[]{:S(2)}) collective-permute-start(bf16[1792,4096]{1,0:T(8,128)(2,1)S(1)} %get-tuple-element.16), channel_id=1, source_target_pairs={{0,24},{8,0},{16,8},{24,16},{1,25},{9,1},{17,9},{25,17},{2,26},{10... | collective-permute-start | bytes 44040200 | tf_op jit(solution)/shard_map/cond/branch_2_fun/ppermute | solution.py:23
  134.7 631.4 %collective-permute-start.7 = (bf16[1792,4096]{1,0:T(8,128)(2,1)S(1)}, bf16[1792,4096]{1,0:T(8,128)(2,1)}, u32[]{:S(2)}, u32[]{:S(2)}) collective-permute-start(bf16[1792,4096]{1,0:T(8,128)(2,1)S(1)} %get-tuple-element.16), channel_id=1, source_target_pairs={{0,8},{8,16},{16,24},{24,0},{1,9},{9,17},{17,25},{25,1},{2,10},{10... | collective-permute-start | bytes 44040200 | tf_op jit(solution)/shard_map/cond/branch_2_fun/ppermute | solution.py:23
  134.7 629.7 %collective-permute-start.8 = (f32[1]{0:T(128)}, f32[1]{0:T(128)}, u32[]{:S(2)}, u32[]{:S(2)}) collective-permute-start(f32[1]{0:T(128)} %get-tuple-element.17), channel_id=1, source_target_pairs={{0,24},{8,0},{16,8},{24,16},{1,25},{9,1},{17,9},{25,17},{2,26},{10... | collective-permute-start | bytes 20 | tf_op jit(solution)/shard_map/cond/branch_2_fun/ppermute | solution.py:23
  138.5 626.9 %collective-permute-start.9 = (f32[1]{0:T(128)}, f32[1]{0:T(128)}, u32[]{:S(2)}, u32[]{:S(2)}) collective-permute-start(f32[1]{0:T(128)} %get-tuple-element.17), channel_id=1, source_target_pairs={{0,8},{8,16},{16,24},{24,0},{1,9},{9,17},{17,25},{25,1},{2,10},{10... | collective-permute-start | bytes 20 | tf_op jit(solution)/shard_map/cond/branch_2_fun/ppermute | solution.py:23
Sparse Core Ops, SparseCore 0:
  9.9 88.3 all-gather.2
where the time goes:
time: 812 us; the launch traced here: 811 us
  waiting for transfers between devices  697 us (86%)
  other arithmetic  37.3 us (5%)
  matrix products  26.8 us (3%)
  local copies, waits for them, and re-layouts  18.7 us (2%)
  between operations  17.2 us (2%)
  starting transfers between devices  13.1 us (2%)
    ppermute x4, waiting for transfers between devices, shifted(): return lax.ppermute(value, axis, pairs)  626 us
    all_to_all x1, waiting for transfers between devices, per_device(): lax.all_to_all(acts, 'node', split_axis=1, concat_axis=0, tiled=True)  51.6 us
    dot_general x1, matrix products, per_device(): lax.dot_general(columns, lax.all_gather(cots, 'node', axis=0, tiled=True)...  26.8 us
    broadcast_in_dim x1, other arithmetic, per_device(): return (mixed[None], new_weight)  20.3 us
    all_gather x1, waiting for transfers between devices, per_device(): lax.all_gather(cots, 'node', axis=0, tiled=True)  18.4 us
    add x1, other arithmetic, neighbours(): back_share * behind.astype(jnp.float32)  17 us
  transfers between devices with their start and end apart: 6, of which 4 were waited for; matrix products, arithmetic and copies ran while one was open for 2% of the time, Pallas kernels for 0%

commit v1 on v0

v1 whole, which is shorter than its diff:
```python
import jax
import jax.numpy as jnp
from jax import lax
from jax.sharding import PartitionSpec as P

base_rate = 40.0
moment_decay = 0.9
keep_share = 0.5
back_share = 0.3
front_share = 0.2
tokens_axis = (((0,), (0,)), ((), ()))
target_chunks = 8


def shifted(value, axis, steps):
    count = lax.axis_size(axis)
    pairs = [(source, (source + steps) % count) for source in range(count)]
    return lax.ppermute(value, axis, pairs)


def chunk_count(rows):
    for count in range(target_chunks, 0, -1):
        if rows % count == 0 and (rows // count) % 16 == 0:
            return count
    return 1


def pipeline(amount, groups, chunks, params, momentum, acts, cots, push_weight, rate):
    tok_group = cots.shape[0]
    size = params.shape[1] // chunks
    paired = (2 * amount) % groups == 0
    outs = []
    for k in range(chunks):
        cols = lax.all_to_all(acts[:, :, k, :], "node", split_axis=1, concat_axis=0, tiled=True)
        cols = cols.reshape(tok_group, size)
        grad = lax.dot_general(cols, cots, tokens_axis, preferred_element_type=jnp.float32)
        grad = grad / tok_group
        rows = slice(k * size, (k + 1) * size)
        renewed = moment_decay * momentum[0, rows].astype(jnp.float32) + grad
        half = (params[0, rows].astype(jnp.float32) - rate * renewed).astype(jnp.bfloat16)
        behind = shifted(half, "grp", amount)
        ahead = behind if paired else shifted(half, "grp", groups - amount)
        total = (
            keep_share * half.astype(jnp.float32)
            + back_share * behind.astype(jnp.float32)
            + front_share * ahead.astype(jnp.float32)
        )
        outs.append(total.astype(jnp.bfloat16))
    mixed = jnp.concatenate(outs, axis=0)
    weight_behind = shifted(push_weight, "grp", amount)
    weight_ahead = shifted(push_weight, "grp", groups - amount)
    new_weight = keep_share * push_weight + back_share * weight_behind + front_share * weight_ahead
    return mixed[None], new_weight


def per_device(params, momentum, hidden, cotangent, push_weight, offsets, step):
    groups = lax.axis_size("grp")
    nodes = lax.axis_size("node")
    position = step[0]
    offset = offsets[position]
    rate = base_rate * (1.0 - 0.5 * position.astype(jnp.float32) / offsets.shape[0])
    cots = lax.all_gather(cotangent[0], "node", axis=0, tiled=True)
    chunks = chunk_count(params.shape[1])
    size = params.shape[1] // chunks
    acts = hidden[0].reshape(hidden.shape[1], nodes, chunks, size)
    branches = [
        (lambda *a, amount=amount: pipeline(amount, groups, chunks, *a))
        for amount in range(1, groups)
    ]
    return lax.switch(offset - 1, branches, params, momentum, acts, cots, push_weight, rate)


def solution(mesh):
    in_specs = (
        P("grp", "node", None),
        P("grp", "node", None),
        P("grp", "node", None),
        P("grp", "node", None),
        P("grp"),
        P(),
        P(),
    )
    out_specs = (P("grp", "node", None), P("grp"))
    return jax.shard_map(
        per_device, mesh=mesh, in_specs=in_specs, out_specs=out_specs, check_vma=False
    )
```

time: 812 us -> 789 us (0.972)
  waiting for transfers between devices: 697 us -> 591 us
  matrix products: 26.8 us -> 62.7 us
  starting transfers between devices: 13.1 us -> 39.2 us
  loops' own time: 1.27 us -> 23.7 us
  other arithmetic: 37.3 us -> 16.9 us
  blocking collectives: 0 us -> 11.6 us
    ppermute x4 -> x9, waiting for transfers between devices: 626 us -> 531 us  [shifted(): return lax.ppermute(value, axis, pairs)]
    all_to_all x1 -> x7, waiting for transfers between devices: 51.6 us -> 3.35 us  [pipeline(): lax.all_to_all(acts[:, :, k, :], 'node', split_axis=1, concat_axis=0, til...]
    all_gather x1, waiting for transfers between devices: 18.4 us -> 56.6 us  [per_device(): cots = lax.all_gather(cotangent[0], 'node', axis=0, tiled=True)]
    dot_general x1 -> x8, matrix products: 26.8 us -> 62.7 us  [pipeline(): lax.dot_general(cols, cots, tokens_axis, preferred_element_type=jnp.float32)]
    all_to_all x1 -> x7, starting transfers between devices: 5.17 us -> 28.3 us  [pipeline(): lax.all_to_all(acts[:, :, k, :], 'node', split_axis=1, concat_axis=0, til...]
    another operation x1, loops' own time: 1.27 us -> 23.7 us  [per_device(): lax.switch(offset - 1, branches, params, momentum, acts, cots, push_weigh...]
    broadcast_in_dim x1 -> x0, other arithmetic: 20.3 us -> none  [per_device(): return (mixed[None], new_weight)]
    add x1 -> x0, other arithmetic: 17 us -> none  [neighbours(): back_share * behind.astype(jnp.float32)]
  transfers between devices with their start and end apart: 6 -> 17, of which waited for: 4 -> 12; matrix products, arithmetic and copies ran while one was open for 2% -> 10% of each run, Pallas kernels for 0% -> 0%
where the time goes in v1:
time: 789 us; the launch traced here: 780 us
  waiting for transfers between devices  591 us (75%)
  matrix products  62.7 us (8%)
  starting transfers between devices  39.2 us (5%)
  loops' own time  23.7 us (3%)
  local copies, waits for them, and re-layouts  17.9 us (2%)
  between operations  17 us (2%)
  other arithmetic  16.9 us (2%)
  blocking collectives  11.6 us (1%)
    ppermute x9, waiting for transfers between devices, shifted(): return lax.ppermute(value, axis, pairs)  531 us
    dot_general x8, matrix products, pipeline(): lax.dot_general(cols, cots, tokens_axis, preferred_element_type=jnp.float32)  62.7 us
    all_gather x1, waiting for transfers between devices, per_device(): cots = lax.all_gather(cotangent[0], 'node', axis=0, tiled=True)  56.6 us
    all_to_all x7, starting transfers between devices, pipeline(): lax.all_to_all(acts[:, :, k, :], 'node', split_axis=1, concat_axis=0, til...  28.3 us
    another operation x1, loops' own time, per_device(): lax.switch(offset - 1, branches, params, momentum, acts, cots, push_weigh...  23.7 us
    cond x7, other arithmetic  16 us
  transfers between devices with their start and end apart: 17, of which 12 were waited for; matrix products, arithmetic and copies ran while one was open for 10% of the time, Pallas kernels for 0%

profile of v1, /device:TPU:0, one launch (start us, length us, event | category | flops | bytes accessed | tf_op | source)
XLA Modules:
  0.0 780.3 jit_solution(16675867679361931130)
XLA Ops:
  10.4 56.6 %all-gather.3.cloned.1.call-done = bf16[1,1024,4096]{2,1,0:T(8,128)(2,1)} async-done(((bf16[1,128,4096]{2,1,0:T(8,128)(2,1)}), bf16[1,1024,4096]{2,1,0:T(8,128)(2,1)}) %all-gather.3.cloned.1.call-update) | async-done | bytes 8388624 | tf_op jit(solution)/shard_map/all_gather | solution.py:62
  67.0 704.9 %conditional.1 = (bf16[1,1792,4096]{2,1,0:T(8,128)(2,1)}, f32[1]{0:T(128)}) conditional(s32[]{:T(128)} %bitcast.127, (bf16[1,1792,4096]{2,1,0:T(8,128)(2,1)}, (), bf16[1,1792,4096]{2,1,0:T(8,128)(2,1)}, bf16[1,128,14336]{2,1,0:T(8,128)(2,1)}, bf16[1024,4096]{1,0:T(8,128)(2,1)}, /*index=5*/f32[1]{0:T(128)}, (), s32[]{:T(128)}, ...), branch_computations={%region_0.0_spmd, %region_1.0_spmd, %region_2.0_spmd} | conditional | flops 15157166080 | bytes 345572416 | solution.py:70
  74.3 6.1 copy.52
  84.1 11.6 %all_to_all.289 = bf16[128,8,224]{0,2,1:T(8,128)(2,1)S(1)} all-to-all(bf16[128,8,224]{0,2,1:T(8,128)(2,1)S(1)} %get-tuple-element.148), channel_id=1, replica_groups=mesh['grp'=4,'node'=8] {'node'}, dimensions={1} | all-to-all | bytes 917504 | tf_op jit(solution)/shard_map/cond/branch_1_fun/all_to_all | solution.py:34
  111.6 7.0 fusion.87
  125.5 8.2 %fusion.86 = bf16[224,4096]{1,0:T(8,128)(2,1)} fusion(bf16[1024,4096]{1,0:T(8,128)(2,1)} %get-tuple-element.46, bf16[1,1792,4096]{2,1,0:T(8,128)(2,1)} %get-tuple-element.86, bf16[1,1792,4096]{2,1,0:T(8,128)(2,1)} %get-tuple-element.77, f32[]{:T(128)S(6)} %mul_shard_map.5, bf16[28,8,8,128]{3,2,1,0:T(8,128)(2,1)S(1)} %bitcast.480), kind=kOutput, calls=%fused_computation.118 | convolution fusion | flops 1886388224 | bytes 14352388 | tf_op jit(solution)/shard_map/cond/branch_1_fun/dot_general | solution.py:36
  139.1 8.2 %fusion.85 = bf16[224,4096]{1,0:T(8,128)(2,1)} fusion(bf16[1024,4096]{1,0:T(8,128)(2,1)} %get-tuple-element.46, bf16[1,1792,4096]{2,1,0:T(8,128)(2,1)} %get-tuple-element.86, bf16[1,1792,4096]{2,1,0:T(8,128)(2,1)} %get-tuple-element.77, f32[]{:T(128)S(6)} %mul_shard_map.5, bf16[28,8,8,128]{3,2,1,0:T(8,128)(2,1)S(1)} %bitcast.481), kind=kOutput, calls=%fused_computation.117 | convolution fusion | flops 1886388224 | bytes 14352388 | tf_op jit(solution)/shard_map/cond/branch_1_fun/dot_general | solution.py:36
  149.5 4.6 all-to-all-start.13
  154.1 8.3 %fusion.84 = bf16[224,4096]{1,0:T(8,128)(2,1)} fusion(bf16[1024,4096]{1,0:T(8,128)(2,1)} %get-tuple-element.46, bf16[1,1792,4096]{2,1,0:T(8,128)(2,1)} %get-tuple-element.86, bf16[1,1792,4096]{2,1,0:T(8,128)(2,1)} %get-tuple-element.77, f32[]{:T(128)S(6)} %mul_shard_map.5, bf16[28,8,8,128]{3,2,1,0:T(8,128)(2,1)S(1)} %bitcast.482), kind=kOutput, calls=%fused_computation.116 | convolution fusion | flops 1886388224 | bytes 14352388 | tf_op jit(solution)/shard_map/cond/branch_1_fun/dot_general | solution.py:36
  163.6 4.2 all-to-all-start.14
  167.8 8.3 %fusion.83 = bf16[224,4096]{1,0:T(8,128)(2,1)} fusion(bf16[1024,4096]{1,0:T(8,128)(2,1)} %get-tuple-element.46, bf16[1,1792,4096]{2,1,0:T(8,128)(2,1)} %get-tuple-element.86, bf16[1,1792,4096]{2,1,0:T(8,128)(2,1)} %get-tuple-element.77, f32[]{:T(128)S(6)} %mul_shard_map.5, bf16[28,8,8,128]{3,2,1,0:T(8,128)(2,1)S(1)} %bitcast.483), kind=kOutput, calls=%fused_computation.115 | convolution fusion | flops 1886388224 | bytes 14352388 | tf_op jit(solution)/shard_map/cond/branch_1_fun/dot_general | solution.py:36
  178.2 4.2 all-to-all-start.15
  182.4 8.3 %fusion.82 = bf16[224,4096]{1,0:T(8,128)(2,1)} fusion(bf16[1024,4096]{1,0:T(8,128)(2,1)} %get-tuple-element.46, bf16[1,1792,4096]{2,1,0:T(8,128)(2,1)} %get-tuple-element.86, bf16[1,1792,4096]{2,1,0:T(8,128)(2,1)} %get-tuple-element.77, f32[]{:T(128)S(6)} %mul_shard_map.5, bf16[28,8,8,128]{3,2,1,0:T(8,128)(2,1)S(1)} %bitcast.472), kind=kOutput, calls=%fused_computation.114 | convolution fusion | flops 1886388224 | bytes 14352388 | tf_op jit(solution)/shard_map/cond/branch_1_fun/dot_general | solution.py:36
  191.6 7.2 fusion.81
  198.8 7.1 fusion.80
  206.0 153.2 %collective-permute-done.18 = bf16[224,4096]{1,0:T(8,128)(2,1)} collective-permute-done((bf16[224,4096]{1,0:T(8,128)(2,1)S(1)}, bf16[224,4096]{1,0:T(8,128)(2,1)}, u32[]{:S(2)}, u32[]{:S(2)}) %collective-permute-start.18) | collective-permute-done | bytes 1835040 | tf_op jit(solution)/shard_map/cond/branch_1_fun/ppermute | solution.py:18
  361.6 76.2 %collective-permute-done.19 = bf16[224,4096]{1,0:T(8,128)(2,1)} collective-permute-done((bf16[224,4096]{1,0:T(8,128)(2,1)}, bf16[224,4096]{1,0:T(8,128)(2,1)}, u32[]{:S(2)}, u32[]{:S(2)}) %collective-permute-start.19) | collective-permute-done | bytes 1835040 | tf_op jit(solution)/shard_map/cond/branch_1_fun/ppermute | solution.py:18
  440.8 75.7 %collective-permute-done.20 = bf16[224,4096]{1,0:T(8,128)(2,1)} collective-permute-done((bf16[224,4096]{1,0:T(8,128)(2,1)}, bf16[224,4096]{1,0:T(8,128)(2,1)}, u32[]{:S(2)}, u32[]{:S(2)}) %collective-permute-start.20) | collective-permute-done | bytes 1835040 | tf_op jit(solution)/shard_map/cond/branch_1_fun/ppermute | solution.py:18
  519.4 75.7 %collective-permute-done.21 = bf16[224,4096]{1,0:T(8,128)(2,1)} collective-permute-done((bf16[224,4096]{1,0:T(8,128)(2,1)}, bf16[224,4096]{1,0:T(8,128)(2,1)}, u32[]{:S(2)}, u32[]{:S(2)}) %collective-permute-start.21) | collective-permute-done | bytes 1835040 | tf_op jit(solution)/shard_map/cond/branch_1_fun/ppermute | solution.py:18
  598.1 36.4 %collective-permute-done.22 = bf16[224,4096]{1,0:T(8,128)(2,1)} collective-permute-done((bf16[224,4096]{1,0:T(8,128)(2,1)}, bf16[224,4096]{1,0:T(8,128)(2,1)}, u32[]{:S(2)}, u32[]{:S(2)}) %collective-permute-start.22) | collective-permute-done | bytes 1835040 | tf_op jit(solution)/shard_map/cond/branch_1_fun/ppermute | solution.py:18
  637.4 36.3 %collective-permute-done.23 = bf16[224,4096]{1,0:T(8,128)(2,1)S(1)} collective-permute-done((bf16[224,4096]{1,0:T(8,128)(2,1)S(1)}, bf16[224,4096]{1,0:T(8,128)(2,1)S(1)}, u32[]{:S(2)}, u32[]{:S(2)}) %collective-permute-start.23) | collective-permute-done | bytes 1835040 | tf_op jit(solution)/shard_map/cond/branch_1_fun/ppermute | solution.py:18
  674.6 38.4 %collective-permute-done.24 = bf16[224,4096]{1,0:T(8,128)(2,1)S(1)} collective-permute-done((bf16[224,4096]{1,0:T(8,128)(2,1)S(1)}, bf16[224,4096]{1,0:T(8,128)(2,1)S(1)}, u32[]{:S(2)}, u32[]{:S(2)}) %collective-permute-start.24) | collective-permute-done | bytes 1835040 | tf_op jit(solution)/shard_map/cond/branch_1_fun/ppermute | solution.py:18
  713.9 38.0 %collective-permute-done.25 = bf16[224,4096]{1,0:T(8,128)(2,1)S(1)} collective-permute-done((bf16[224,4096]{1,0:T(8,128)(2,1)S(1)}, bf16[224,4096]{1,0:T(8,128)(2,1)S(1)}, u32[]{:S(2)}, u32[]{:S(2)}) %collective-permute-start.25) | collective-permute-done | bytes 1835040 | tf_op jit(solution)/shard_map/cond/branch_1_fun/ppermute | solution.py:18
  752.8 5.5 copy-done.7
  (44 shorter events, 54.4 us)
Async XLA Ops:
  7.2 59.8 %all-gather.3.cloned.1.call-start = ((), (), s32[]{:S(2)}) async-start(), calls=%async_computation.24 | async-start | bytes 9437184 | tf_op jit(solution)/shard_map/all_gather | solution.py:62
  95.7 12.5 %all-to-all-start.9 = ((bf16[128,8,224]{0,2,1:T(8,128)(2,1)}), bf16[128,8,224]{0,2,1:T(8,128)(2,1)S(1)}, u32[]{:S(2)}, u32[]{:S(2)}) async-start(bf16[128,8,224]{0,2,1:T(8,128)(2,1)} %get-tuple-element.147), calls=%async_computation.9 | async-start | bytes 917504 | tf_op jit(solution)/shard_map/cond/branch_1_fun/all_to_all | solution.py:34
  99.2 4.7 collective-permute-start.26
  108.2 13.2 %all-to-all-start.10 = ((bf16[128,8,224]{0,2,1:T(8,128)(2,1)}), bf16[128,8,224]{0,2,1:T(8,128)(2,1)S(1)}, u32[]{:S(2)}, u32[]{:S(2)}) async-start(bf16[128,8,224]{0,2,1:T(8,128)(2,1)} %get-tuple-element.146), calls=%async_computation.10 | async-start | bytes 917504 | tf_op jit(solution)/shard_map/cond/branch_1_fun/all_to_all | solution.py:34
  118.7 240.5 %collective-permute-start.18 = (bf16[224,4096]{1,0:T(8,128)(2,1)S(1)}, bf16[224,4096]{1,0:T(8,128)(2,1)}, u32[]{:S(2)}, u32[]{:S(2)}) collective-permute-start(bf16[224,4096]{1,0:T(8,128)(2,1)S(1)} %fusion.87), channel_id=1, source_target_pairs={{0,16},{8,24},{16,0},{24,8},{1,17},{9,25},{17,1},{25,9},{2,18},{10... | collective-permute-start | bytes 5505032 | tf_op jit(solution)/shard_map/cond/branch_1_fun/ppermute | solution.py:18
  121.3 13.6 %all-to-all-start.11 = ((bf16[128,8,224]{0,2,1:T(8,128)(2,1)}), bf16[128,8,224]{0,2,1:T(8,128)(2,1)S(1)}, u32[]{:S(2)}, u32[]{:S(2)}) async-start(bf16[128,8,224]{0,2,1:T(8,128)(2,1)} %get-tuple-element.145), calls=%async_computation.11 | async-start | bytes 917504 | tf_op jit(solution)/shard_map/cond/branch_1_fun/all_to_all | solution.py:34
  133.7 304.1 %collective-permute-start.19 = (bf16[224,4096]{1,0:T(8,128)(2,1)}, bf16[224,4096]{1,0:T(8,128)(2,1)}, u32[]{:S(2)}, u32[]{:S(2)}) collective-permute-start(bf16[224,4096]{1,0:T(8,128)(2,1)} %fusion.86), channel_id=1, source_target_pairs={{0,16},{8,24},{16,0},{24,8},{1,17},{9,25},{17,1},{25,9},{2,18},{10... | collective-permute-start | bytes 5505032 | tf_op jit(solution)/shard_map/cond/branch_1_fun/ppermute | solution.py:18
  134.9 14.5 %all-to-all-start.12 = ((bf16[128,8,224]{0,2,1:T(8,128)(2,1)}), bf16[128,8,224]{0,2,1:T(8,128)(2,1)S(1)}, u32[]{:S(2)}, u32[]{:S(2)}) async-start(bf16[128,8,224]{0,2,1:T(8,128)(2,1)} %get-tuple-element.144), calls=%async_computation.12 | async-start | bytes 917504 | tf_op jit(solution)/shard_map/cond/branch_1_fun/all_to_all | solution.py:34
  147.3 369.2 %collective-permute-start.20 = (bf16[224,4096]{1,0:T(8,128)(2,1)}, bf16[224,4096]{1,0:T(8,128)(2,1)}, u32[]{:S(2)}, u32[]{:S(2)}) collective-permute-start(bf16[224,4096]{1,0:T(8,128)(2,1)} %fusion.85), channel_id=1, source_target_pairs={{0,16},{8,24},{16,0},{24,8},{1,17},{9,25},{17,1},{25,9},{2,18},{10... | collective-permute-start | bytes 5505032 | tf_op jit(solution)/shard_map/cond/branch_1_fun/ppermute | solution.py:18
  149.5 14.1 %all-to-all-start.13 = ((bf16[128,8,224]{0,2,1:T(8,128)(2,1)}), bf16[128,8,224]{0,2,1:T(8,128)(2,1)S(1)}, u32[]{:S(2)}, u32[]{:S(2)}) async-start(bf16[128,8,224]{0,2,1:T(8,128)(2,1)} %get-tuple-element.143), calls=%async_computation.13 | async-start | bytes 917504 | tf_op jit(solution)/shard_map/cond/branch_1_fun/all_to_all | solution.py:34
  162.4 432.7 %collective-permute-start.21 = (bf16[224,4096]{1,0:T(8,128)(2,1)}, bf16[224,4096]{1,0:T(8,128)(2,1)}, u32[]{:S(2)}, u32[]{:S(2)}) collective-permute-start(bf16[224,4096]{1,0:T(8,128)(2,1)} %fusion.84), channel_id=1, source_target_pairs={{0,16},{8,24},{16,0},{24,8},{1,17},{9,25},{17,1},{25,9},{2,18},{10... | collective-permute-start | bytes 5505032 | tf_op jit(solution)/shard_map/cond/branch_1_fun/ppermute | solution.py:18
  163.6 14.6 %all-to-all-start.14 = ((bf16[128,8,224]{0,2,1:T(8,128)(2,1)}), bf16[128,8,224]{0,2,1:T(8,128)(2,1)S(1)}, u32[]{:S(2)}, u32[]{:S(2)}) async-start(bf16[128,8,224]{0,2,1:T(8,128)(2,1)} %get-tuple-element.142), calls=%async_computation.14 | async-start | bytes 917504 | tf_op jit(solution)/shard_map/cond/branch_1_fun/all_to_all | solution.py:34
  176.0 458.4 %collective-permute-start.22 = (bf16[224,4096]{1,0:T(8,128)(2,1)}, bf16[224,4096]{1,0:T(8,128)(2,1)}, u32[]{:S(2)}, u32[]{:S(2)}) collective-permute-start(bf16[224,4096]{1,0:T(8,128)(2,1)} %fusion.83), channel_id=1, source_target_pairs={{0,16},{8,24},{16,0},{24,8},{1,17},{9,25},{17,1},{25,9},{2,18},{10... | collective-permute-start | bytes 5505032 | tf_op jit(solution)/shard_map/cond/branch_1_fun/ppermute | solution.py:18
  178.2 13.3 %all-to-all-start.15 = ((bf16[128,8,224]{0,2,1:T(8,128)(2,1)}), bf16[128,8,224]{0,2,1:T(8,128)(2,1)S(1)}, u32[]{:S(2)}, u32[]{:S(2)}) async-start(bf16[128,8,224]{0,2,1:T(8,128)(2,1)} %get-tuple-element.141), calls=%async_computation.15 | async-start | bytes 917504 | tf_op jit(solution)/shard_map/cond/branch_1_fun/all_to_all | solution.py:34
  198.8 160.4 %copy-start.6 = (bf16[224,4096]{1,0:T(8,128)(2,1)S(1)}, bf16[224,4096]{1,0:T(8,128)(2,1)}, u32[]{:S(2)}) copy-start(bf16[224,4096]{1,0:T(8,128)(2,1)} %fusion.82) | copy-start | bytes 5505028 | tf_op jit(solution)/shard_map/cond
  359.2 314.5 %collective-permute-start.23 = (bf16[224,4096]{1,0:T(8,128)(2,1)S(1)}, bf16[224,4096]{1,0:T(8,128)(2,1)S(1)}, u32[]{:S(2)}, u32[]{:S(2)}) collective-permute-start(bf16[224,4096]{1,0:T(8,128)(2,1)S(1)} %copy-done.6), channel_id=1, source_target_pairs={{0,16},{8,24},{16,0},{24,8},{1,17},{9,25},{17,1},{25,9},{2,18},{10... | collective-permute-start | bytes 5505032 | tf_op jit(solution)/shard_map/cond/branch_1_fun/ppermute | solution.py:18
  437.8 275.2 %collective-permute-start.24 = (bf16[224,4096]{1,0:T(8,128)(2,1)S(1)}, bf16[224,4096]{1,0:T(8,128)(2,1)S(1)}, u32[]{:S(2)}, u32[]{:S(2)}) collective-permute-start(bf16[224,4096]{1,0:T(8,128)(2,1)S(1)} %fusion.81), channel_id=1, source_target_pairs={{0,16},{8,24},{16,0},{24,8},{1,17},{9,25},{17,1},{25,9},{2,18},{10... | collective-permute-start | bytes 5505032 | tf_op jit(solution)/shard_map/cond/branch_1_fun/ppermute | solution.py:18
  516.5 235.4 %collective-permute-start.25 = (bf16[224,4096]{1,0:T(8,128)(2,1)S(1)}, bf16[224,4096]{1,0:T(8,128)(2,1)S(1)}, u32[]{:S(2)}, u32[]{:S(2)}) collective-permute-start(bf16[224,4096]{1,0:T(8,128)(2,1)S(1)} %fusion.80), channel_id=1, source_target_pairs={{0,16},{8,24},{16,0},{24,8},{1,17},{9,25},{17,1},{25,9},{2,18},{10... | collective-permute-start | bytes 5505032 | tf_op jit(solution)/shard_map/cond/branch_1_fun/ppermute | solution.py:18
  752.7 5.5 copy-start.7
Sparse Core Ops, SparseCore 0:
  9.9 57.0 all-gather.2

commit v2 on v1

v2 whole, which is shorter than its diff:
```python
import jax
import jax.numpy as jnp
from jax import lax
from jax.sharding import PartitionSpec as P

base_rate = 40.0
moment_decay = 0.9
keep_share = 0.5
back_share = 0.3
front_share = 0.2
tokens_axis = (((0,), (0,)), ((), ()))
row_blocks = 4
col_blocks = 4


def shifted(value, axis, steps):
    count = lax.axis_size(axis)
    pairs = [(source, (source + steps) % count) for source in range(count)]
    return lax.ppermute(value, axis, pairs)


def block_count(length, target, quantum):
    for count in range(target, 0, -1):
        if length % count == 0 and (length // count) % quantum == 0:
            return count
    return 1


def pipeline(amount, groups, params, momentum, acts, cotangent, push_weight, rate, direct):
    n_rows, row_size = acts.shape[2], acts.shape[3]
    width = cotangent.shape[1]
    n_cols = block_count(width, col_blocks, 128)
    col_size = width // n_cols
    paired = (2 * amount) % groups == 0
    w_minus = jnp.where(direct, back_share, front_share).astype(jnp.float32)
    w_plus = jnp.where(direct, front_share, back_share).astype(jnp.float32)
    cots = [None] * n_cols
    row_parts = []
    for a in range(n_rows):
        col_parts = []
        cols = lax.all_to_all(acts[:, :, a, :], "node", split_axis=1, concat_axis=0, tiled=True)
        cols = cols.reshape(-1, row_size)
        tok_group = cols.shape[0]
        rows = slice(a * row_size, (a + 1) * row_size)
        for b in range(n_cols):
            span = slice(b * col_size, (b + 1) * col_size)
            if cots[b] is None:
                cots[b] = lax.all_gather(cotangent[:, span], "node", axis=0, tiled=True)
            grad = lax.dot_general(cols, cots[b], tokens_axis, preferred_element_type=jnp.float32)
            grad = grad / tok_group
            renewed = moment_decay * momentum[0, rows, span].astype(jnp.float32) + grad
            half = (params[0, rows, span].astype(jnp.float32) - rate * renewed).astype(jnp.bfloat16)
            minus = shifted(half, "grp", amount)
            if paired:
                peers = (back_share * minus.astype(jnp.float32)) + front_share * minus.astype(jnp.float32)
            else:
                plus = shifted(half, "grp", groups - amount)
                peers = w_minus * minus.astype(jnp.float32) + w_plus * plus.astype(jnp.float32)
            total = keep_share * half.astype(jnp.float32) + peers
            col_parts.append(total.astype(jnp.bfloat16))
        row_parts.append(jnp.concatenate(col_parts, axis=1))
    mixed = jnp.concatenate(row_parts, axis=0)
    weight_minus = shifted(push_weight, "grp", amount)
    weight_plus = shifted(push_weight, "grp", groups - amount)
    new_weight = keep_share * push_weight + w_minus * weight_minus + w_plus * weight_plus
    return mixed[None], new_weight


def per_device(params, momentum, hidden, cotangent, push_weight, offsets, step):
    groups = lax.axis_size("grp")
    nodes = lax.axis_size("node")
    position = step[0]
    offset = offsets[position]
    rate = base_rate * (1.0 - 0.5 * position.astype(jnp.float32) / offsets.shape[0])
    rows = params.shape[1]
    n_rows = block_count(rows, row_blocks, 16)
    acts = hidden[0].reshape(hidden.shape[1], nodes, n_rows, rows // n_rows)
    amounts = list(range(1, groups // 2 + 1))
    direct = offset <= groups // 2
    index = jnp.where(direct, offset, groups - offset) - 1
    branches = [
        (lambda *a, amount=amount: pipeline(amount, groups, *a))
        for amount in amounts
    ]
    return lax.switch(
        index, branches, params, momentum, acts, cotangent[0], push_weight, rate, direct
    )


def solution(mesh):
    in_specs = (
        P("grp", "node", None),
        P("grp", "node", None),
        P("grp", "node", None),
        P("grp", "node", None),
        P("grp"),
        P(),
        P(),
    )
    out_specs = (P("grp", "node", None), P("grp"))
    return jax.shard_map(
        per_device, mesh=mesh, in_specs=in_specs, out_specs=out_specs, check_vma=False
    )
```

time: 789 us -> 891 us (1.13)
  other arithmetic: 16.9 us -> 142 us
  waiting for transfers between devices: 591 us -> 503 us
  blocking collectives: 11.6 us -> 62.4 us
  starting transfers between devices: 39.2 us -> 75.4 us
  loops' own time: 23.7 us -> 12.2 us
    broadcast_in_dim x0 -> x1, other arithmetic: none -> 119 us  [pipeline(): return (mixed[None], new_weight)]
    ppermute x9 -> x34, starting transfers between devices: 10.9 us -> 71.7 us  [shifted(): return lax.ppermute(value, axis, pairs)]
    ppermute x9 -> x34, waiting for transfers between devices: 531 us -> 477 us  [shifted(): return lax.ppermute(value, axis, pairs)]
    all_to_all x1 -> x3, blocking collectives: 11.6 us -> 62.4 us  [pipeline(): lax.all_to_all(acts[:, :, a, :], 'node', split_axis=1, concat_axis=0, til...]
    all_gather x1 -> x4, waiting for transfers between devices: 56.6 us -> 18.5 us  [pipeline(): cots[b] = lax.all_gather(cotangent[:, span], 'node', axis=0, tiled=True)]
    all_to_all x7 -> x1, starting transfers between devices: 28.3 us -> 3.55 us  [pipeline(): lax.all_to_all(acts[:, :, a, :], 'node', split_axis=1, concat_axis=0, til...]
    convert_element_type x0 -> x16, other arithmetic: none -> 23.4 us  [pipeline(): col_parts.append(total.astype(jnp.bfloat16))]
    cond x7 -> x1, other arithmetic: 16 us -> 0.01 us
  transfers between devices with their start and end apart: 17 -> 39, of which waited for: 12 -> 31; matrix products, arithmetic and copies ran while one was open for 10% -> 9% of each run, Pallas kernels for 0% -> 0%
where the time goes in v2:
time: 891 us; the launch traced here: 884 us
  waiting for transfers between devices  503 us (56%)
  other arithmetic  142 us (16%)
  starting transfers between devices  75.4 us (8%)
  blocking collectives  62.4 us (7%)
  matrix products  54.3 us (6%)
  between operations  17.7 us (2%)
  local copies, waits for them, and re-layouts  16.8 us (2%)
  loops' own time  12.2 us (1%)
    ppermute x34, waiting for transfers between devices, shifted(): return lax.ppermute(value, axis, pairs)  477 us
    broadcast_in_dim x1, other arithmetic, pipeline(): return (mixed[None], new_weight)  119 us
    ppermute x34, starting transfers between devices, shifted(): return lax.ppermute(value, axis, pairs)  71.7 us
    all_to_all x3, blocking collectives, pipeline(): lax.all_to_all(acts[:, :, a, :], 'node', split_axis=1, concat_axis=0, til...  62.4 us
    dot_general x16, matrix products, pipeline(): lax.dot_general(cols, cots[b], tokens_axis, preferred_element_type=jnp.fl...  54.3 us
    convert_element_type x16, other arithmetic, pipeline(): col_parts.append(total.astype(jnp.bfloat16))  23.4 us
    all_gather x4, waiting for transfers between devices, pipeline(): cots[b] = lax.all_gather(cotangent[:, span], 'node', axis=0, tiled=True)  18.5 us
  transfers between devices with their start and end apart: 39, of which 31 were waited for; matrix products, arithmetic and copies ran while one was open for 9% of the time, Pallas kernels for 0%

profile of v2, /device:TPU:0, one launch (start us, length us, event | category | flops | bytes accessed | tf_op | source)
XLA Modules:
  0.0 884.1 jit_solution(4460544983552168686)
XLA Ops:
  11.0 6.2 copy.21
  17.2 859.0 %conditional.1 = (bf16[1,1792,4096]{2,1,0:T(8,128)(2,1)}, f32[1]{0:T(128)}) conditional(s32[]{:T(128)} %clamp.3, (bf16[1,1792,4096]{2,1,0:T(8,128)(2,1)}, f32[]{:T(128)}, bf16[1,1792,4096]{2,1,0:T(8,128)(2,1)}, bf16[128,8,4,448]{0,3,2,1:T(8,128)(2,1)}, bf16[128,4096]{1,0:T(8,128)(2,1)S(1)}, /*index=5*/pred[]{:T(512)}, f32[1]{0:T(128)}) %tuple.53, ...), branch_computations={%region_0.1_spmd, %region_1.2_spmd} | conditional | flops 15392047104 | bytes 462817152 | solution.py:85
  23.0 21.7 %all_to_all.96 = bf16[128,8,448]{0,2,1:T(8,128)(2,1)S(1)} all-to-all(bf16[128,8,448]{0,2,1:T(8,128)(2,1)S(1)} %get-tuple-element.46), channel_id=1, replica_groups=mesh['grp'=4,'node'=8] {'node'}, dimensions={1} | all-to-all | bytes 1835008 | tf_op jit(solution)/shard_map/cond/branch_0_fun/all_to_all | solution.py:41
  44.7 20.8 %all_to_all.97 = bf16[128,8,448]{0,2,1:T(8,128)(2,1)S(1)} all-to-all(bf16[128,8,448]{0,2,1:T(8,128)(2,1)S(1)} %get-tuple-element.47), channel_id=1, replica_groups=mesh['grp'=4,'node'=8] {'node'}, dimensions={1} | all-to-all | bytes 1835008 | tf_op jit(solution)/shard_map/cond/branch_0_fun/all_to_all | solution.py:41
  65.5 19.9 %all_to_all.98 = bf16[128,8,448]{0,2,1:T(8,128)(2,1)} all-to-all(bf16[128,8,448]{0,2,1:T(8,128)(2,1)S(1)} %get-tuple-element.48), channel_id=1, replica_groups=mesh['grp'=4,'node'=8] {'node'}, dimensions={1} | all-to-all | bytes 1835008 | tf_op jit(solution)/shard_map/cond/branch_0_fun/all_to_all | solution.py:41
  102.4 6.0 all-to-all-done.1
  154.8 13.7 %all-gather.13.cloned.1.call-done = bf16[1024,1024]{1,0:T(8,128)(2,1)} async-done(((bf16[128,1024]{1,0:T(8,128)(2,1)}), bf16[1024,1024]{1,0:T(8,128)(2,1)}) %all-gather.13.cloned.1.call-update) | async-done | bytes 2097168 | tf_op jit(solution)/shard_map/cond/branch_0_fun/all_gather | solution.py:48
  201.7 32.9 %collective-permute-done.7 = bf16[448,1024]{1,0:T(8,128)(2,1)} collective-permute-done((bf16[448,1024]{1,0:T(8,128)(2,1)}, bf16[448,1024]{1,0:T(8,128)(2,1)}, u32[]{:S(2)}, u32[]{:S(2)}) %collective-permute-start.7) | collective-permute-done | bytes 917536 | tf_op jit(solution)/shard_map/cond/branch_0_fun/ppermute | solution.py:19
  241.0 32.8 %collective-permute-done.15 = bf16[448,1024]{1,0:T(8,128)(2,1)S(1)} collective-permute-done((bf16[448,1024]{1,0:T(8,128)(2,1)S(1)}, bf16[448,1024]{1,0:T(8,128)(2,1)S(1)}, u32[]{:S(2)}, u32[]{:S(2)}) %collective-permute-start.15) | collective-permute-done | bytes 917536 | tf_op jit(solution)/shard_map/cond/branch_0_fun/ppermute | solution.py:19
  282.5 30.5 %collective-permute-done.17 = bf16[448,1024]{1,0:T(8,128)(2,1)S(1)} collective-permute-done((bf16[448,1024]{1,0:T(8,128)(2,1)S(1)}, bf16[448,1024]{1,0:T(8,128)(2,1)S(1)}, u32[]{:S(2)}, u32[]{:S(2)}) %collective-permute-start.17) | collective-permute-done | bytes 917536 | tf_op jit(solution)/shard_map/cond/branch_0_fun/ppermute | solution.py:19
  321.5 30.8 %collective-permute-done.23 = bf16[448,1024]{1,0:T(8,128)(2,1)S(1)} collective-permute-done((bf16[448,1024]{1,0:T(8,128)(2,1)S(1)}, bf16[448,1024]{1,0:T(8,128)(2,1)S(1)}, u32[]{:S(2)}, u32[]{:S(2)}) %collective-permute-start.23) | collective-permute-done | bytes 917536 | tf_op jit(solution)/shard_map/cond/branch_0_fun/ppermute | solution.py:19
  359.4 32.3 %collective-permute-done.25 = bf16[448,1024]{1,0:T(8,128)(2,1)S(1)} collective-permute-done((bf16[448,1024]{1,0:T(8,128)(2,1)S(1)}, bf16[448,1024]{1,0:T(8,128)(2,1)S(1)}, u32[]{:S(2)}, u32[]{:S(2)}) %collective-permute-start.25) | collective-permute-done | bytes 917536 | tf_op jit(solution)/shard_map/cond/branch_0_fun/ppermute | solution.py:19
  398.0 32.9 %collective-permute-done.31 = bf16[448,1024]{1,0:T(8,128)(2,1)S(1)} collective-permute-done((bf16[448,1024]{1,0:T(8,128)(2,1)S(1)}, bf16[448,1024]{1,0:T(8,128)(2,1)S(1)}, u32[]{:S(2)}, u32[]{:S(2)}) %collective-permute-start.31) | collective-permute-done | bytes 917536 | tf_op jit(solution)/shard_map/cond/branch_0_fun/ppermute | solution.py:19
  437.3 32.9 %collective-permute-done.5 = bf16[448,1024]{1,0:T(8,128)(2,1)S(1)} collective-permute-done((bf16[448,1024]{1,0:T(8,128)(2,1)S(1)}, bf16[448,1024]{1,0:T(8,128)(2,1)S(1)}, u32[]{:S(2)}, u32[]{:S(2)}) %collective-permute-start.5) | collective-permute-done | bytes 917536 | tf_op jit(solution)/shard_map/cond/branch_0_fun/ppermute | solution.py:19
  478.1 31.3 %collective-permute-done.13 = bf16[448,1024]{1,0:T(8,128)(2,1)S(1)} collective-permute-done((bf16[448,1024]{1,0:T(8,128)(2,1)S(1)}, bf16[448,1024]{1,0:T(8,128)(2,1)S(1)}, u32[]{:S(2)}, u32[]{:S(2)}) %collective-permute-start.13) | collective-permute-done | bytes 917536 | tf_op jit(solution)/shard_map/cond/branch_0_fun/ppermute | solution.py:19
  517.5 31.3 %collective-permute-done.21 = bf16[448,1024]{1,0:T(8,128)(2,1)S(1)} collective-permute-done((bf16[448,1024]{1,0:T(8,128)(2,1)S(1)}, bf16[448,1024]{1,0:T(8,128)(2,1)S(1)}, u32[]{:S(2)}, u32[]{:S(2)}) %collective-permute-start.21) | collective-permute-done | bytes 917536 | tf_op jit(solution)/shard_map/cond/branch_0_fun/ppermute | solution.py:19
  556.7 31.3 %collective-permute-done.29 = bf16[448,1024]{1,0:T(8,128)(2,1)S(1)} collective-permute-done((bf16[448,1024]{1,0:T(8,128)(2,1)S(1)}, bf16[448,1024]{1,0:T(8,128)(2,1)S(1)}, u32[]{:S(2)}, u32[]{:S(2)}) %collective-permute-start.29) | collective-permute-done | bytes 917536 | tf_op jit(solution)/shard_map/cond/branch_0_fun/ppermute | solution.py:19
  594.4 32.9 %collective-permute-done.3 = bf16[448,1024]{1,0:T(8,128)(2,1)S(1)} collective-permute-done((bf16[448,1024]{1,0:T(8,128)(2,1)S(1)}, bf16[448,1024]{1,0:T(8,128)(2,1)S(1)}, u32[]{:S(2)}, u32[]{:S(2)}) %collective-permute-start.3) | collective-permute-done | bytes 917536 | tf_op jit(solution)/shard_map/cond/branch_0_fun/ppermute | solution.py:19
  633.7 32.9 %collective-permute-done.11 = bf16[448,1024]{1,0:T(8,128)(2,1)S(1)} collective-permute-done((bf16[448,1024]{1,0:T(8,128)(2,1)S(1)}, bf16[448,1024]{1,0:T(8,128)(2,1)S(1)}, u32[]{:S(2)}, u32[]{:S(2)}) %collective-permute-start.11) | collective-permute-done | bytes 917536 | tf_op jit(solution)/shard_map/cond/branch_0_fun/ppermute | solution.py:19
  673.1 32.8 %collective-permute-done.19 = bf16[448,1024]{1,0:T(8,128)(2,1)S(1)} collective-permute-done((bf16[448,1024]{1,0:T(8,128)(2,1)S(1)}, bf16[448,1024]{1,0:T(8,128)(2,1)S(1)}, u32[]{:S(2)}, u32[]{:S(2)}) %collective-permute-start.19) | collective-permute-done | bytes 917536 | tf_op jit(solution)/shard_map/cond/branch_0_fun/ppermute | solution.py:19
  705.9 5.0 collective-permute-done.18
  712.5 17.1 %collective-permute-done.27 = bf16[448,1024]{1,0:T(8,128)(2,1)S(1)} collective-permute-done((bf16[448,1024]{1,0:T(8,128)(2,1)S(1)}, bf16[448,1024]{1,0:T(8,128)(2,1)S(1)}, u32[]{:S(2)}, u32[]{:S(2)}) %collective-permute-start.27) | collective-permute-done | bytes 917536 | tf_op jit(solution)/shard_map/cond/branch_0_fun/ppermute | solution.py:19
  729.5 16.7 %collective-permute-done.26 = bf16[448,1024]{1,0:T(8,128)(2,1)S(1)} collective-permute-done((bf16[448,1024]{1,0:T(8,128)(2,1)S(1)}, bf16[448,1024]{1,0:T(8,128)(2,1)S(1)}, u32[]{:S(2)}, u32[]{:S(2)}) %collective-permute-start.26) | collective-permute-done | bytes 917536 | tf_op jit(solution)/shard_map/cond/branch_0_fun/ppermute | solution.py:19
  747.8 118.6 %maximum_bitcast_fusion = bf16[1,1792,4096]{2,1,0:T(8,128)(2,1)} fusion(bf16[448,1024]{1,0:T(8,128)(2,1)} %add_convert_fusion, bf16[448,1024]{1,0:T(8,128)(2,1)} %add_convert_fusion.1, bf16[448,1024]{1,0:T(8,128)(2,1)} %add_convert_fusion.2, bf16[448,1024]{1,0:T(8,128)(2,1)S(1)} %add_convert_fusion.3, bf16[448,1024]{1,0:T(8,128)(2,1)S(1)} %add_convert_fusion.4, ...), kind=kLoop, calls=%fused_computation | loop fusion | flops 234881024 | bytes 29360128 | tf_op jit(solution)/shard_map/cond/branch_0_fun/broadcast_in_dim | solution.py:66
  (138 shorter events, 191.1 us)
Async XLA Ops:
  17.2 92.7 %all-gather.9.cloned.1.call-start = ((), (), s32[]{:S(2)}) async-start(), calls=%async_computation.8 | async-start | bytes 2359296 | tf_op jit(solution)/shard_map/cond/branch_0_fun/all_gather | solution.py:48
  18.2 107.4 %all-gather.15.cloned.1.call-start = ((), (), s32[]{:S(2)}) async-start(), calls=%async_computation.11 | async-start | bytes 2359296 | tf_op jit(solution)/shard_map/cond/branch_0_fun/all_gather | solution.py:48
  19.0 119.9 %all-gather.11.cloned.1.call-start = ((), (), s32[]{:S(2)}) async-start(), calls=%async_computation.9 | async-start | bytes 2359296 | tf_op jit(solution)/shard_map/cond/branch_0_fun/all_gather | solution.py:48
  130.0 104.6 %collective-permute-start.7 = (bf16[448,1024]{1,0:T(8,128)(2,1)}, bf16[448,1024]{1,0:T(8,128)(2,1)}, u32[]{:S(2)}, u32[]{:S(2)}) collective-permute-start(bf16[448,1024]{1,0:T(8,128)(2,1)} %fusion.12), channel_id=1, source_target_pairs={{0,24},{8,0},{16,8},{24,16},{1,25},{9,1},{17,9},{25,17},{2,26},{10... | collective-permute-start | bytes 2752520 | tf_op jit(solution)/shard_map/cond/branch_0_fun/ppermute | solution.py:19
  195.3 83.2 %collective-permute-start.14 = (bf16[448,1024]{1,0:T(8,128)(2,1)S(1)}, bf16[448,1024]{1,0:T(8,128)(2,1)S(1)}, u32[]{:S(2)}, u32[]{:S(2)}) collective-permute-start(bf16[448,1024]{1,0:T(8,128)(2,1)S(1)} %fusion.8), channel_id=1, source_target_pairs={{0,8},{8,16},{16,24},{24,0},{1,9},{9,17},{17,25},{25,1},{2,10},{10... | collective-permute-start | bytes 2752520 | tf_op jit(solution)/shard_map/cond/branch_0_fun/ppermute | solution.py:19
  200.3 112.8 %collective-permute-start.17 = (bf16[448,1024]{1,0:T(8,128)(2,1)S(1)}, bf16[448,1024]{1,0:T(8,128)(2,1)S(1)}, u32[]{:S(2)}, u32[]{:S(2)}) collective-permute-start(bf16[448,1024]{1,0:T(8,128)(2,1)S(1)} %fusion.7), channel_id=1, source_target_pairs={{0,24},{8,0},{16,8},{24,16},{1,25},{9,1},{17,9},{25,17},{2,26},{10... | collective-permute-start | bytes 2752520 | tf_op jit(solution)/shard_map/cond/branch_0_fun/ppermute | solution.py:19
  239.5 112.8 %collective-permute-start.23 = (bf16[448,1024]{1,0:T(8,128)(2,1)S(1)}, bf16[448,1024]{1,0:T(8,128)(2,1)S(1)}, u32[]{:S(2)}, u32[]{:S(2)}) collective-permute-start(bf16[448,1024]{1,0:T(8,128)(2,1)S(1)} %fusion.4), channel_id=1, source_target_pairs={{0,24},{8,0},{16,8},{24,16},{1,25},{9,1},{17,9},{25,17},{2,26},{10... | collective-permute-start | bytes 2752520 | tf_op jit(solution)/shard_map/cond/branch_0_fun/ppermute | solution.py:19
  278.5 113.1 %collective-permute-start.25 = (bf16[448,1024]{1,0:T(8,128)(2,1)S(1)}, bf16[448,1024]{1,0:T(8,128)(2,1)S(1)}, u32[]{:S(2)}, u32[]{:S(2)}) collective-permute-start(bf16[448,1024]{1,0:T(8,128)(2,1)S(1)} %fusion.3), channel_id=1, source_target_pairs={{0,24},{8,0},{16,8},{24,16},{1,25},{9,1},{17,9},{25,17},{2,26},{10... | collective-permute-start | bytes 2752520 | tf_op jit(solution)/shard_map/cond/branch_0_fun/ppermute | solution.py:19
  317.2 113.7 %collective-permute-start.31 = (bf16[448,1024]{1,0:T(8,128)(2,1)S(1)}, bf16[448,1024]{1,0:T(8,128)(2,1)S(1)}, u32[]{:S(2)}, u32[]{:S(2)}) collective-permute-start(bf16[448,1024]{1,0:T(8,128)(2,1)S(1)} %fusion), channel_id=1, source_target_pairs={{0,24},{8,0},{16,8},{24,16},{1,25},{9,1},{17,9},{25,17},{2,26},{10... | collective-permute-start | bytes 2752520 | tf_op jit(solution)/shard_map/cond/branch_0_fun/ppermute | solution.py:19
  356.6 113.6 %collective-permute-start.5 = (bf16[448,1024]{1,0:T(8,128)(2,1)S(1)}, bf16[448,1024]{1,0:T(8,128)(2,1)S(1)}, u32[]{:S(2)}, u32[]{:S(2)}) collective-permute-start(bf16[448,1024]{1,0:T(8,128)(2,1)S(1)} %fusion.13), channel_id=1, source_target_pairs={{0,24},{8,0},{16,8},{24,16},{1,25},{9,1},{17,9},{25,17},{2,26},{10... | collective-permute-start | bytes 2752520 | tf_op jit(solution)/shard_map/cond/branch_0_fun/ppermute | solution.py:19
  391.6 83.1 %collective-permute-start.4 = (bf16[448,1024]{1,0:T(8,128)(2,1)S(1)}, bf16[448,1024]{1,0:T(8,128)(2,1)S(1)}, u32[]{:S(2)}, u32[]{:S(2)}) collective-permute-start(bf16[448,1024]{1,0:T(8,128)(2,1)S(1)} %fusion.13), channel_id=1, source_target_pairs={{0,8},{8,16},{16,24},{24,0},{1,9},{9,17},{17,25},{25,1},{2,10},{10... | collective-permute-start | bytes 2752520 | tf_op jit(solution)/shard_map/cond/branch_0_fun/ppermute | solution.py:19
  395.9 113.5 %collective-permute-start.13 = (bf16[448,1024]{1,0:T(8,128)(2,1)S(1)}, bf16[448,1024]{1,0:T(8,128)(2,1)S(1)}, u32[]{:S(2)}, u32[]{:S(2)}) collective-permute-start(bf16[448,1024]{1,0:T(8,128)(2,1)S(1)} %fusion.9), channel_id=1, source_target_pairs={{0,24},{8,0},{16,8},{24,16},{1,25},{9,1},{17,9},{25,17},{2,26},{10... | collective-permute-start | bytes 2752520 | tf_op jit(solution)/shard_map/cond/branch_0_fun/ppermute | solution.py:19
  430.9 83.2 %collective-permute-start.12 = (bf16[448,1024]{1,0:T(8,128)(2,1)S(1)}, bf16[448,1024]{1,0:T(8,128)(2,1)S(1)}, u32[]{:S(2)}, u32[]{:S(2)}) collective-permute-start(bf16[448,1024]{1,0:T(8,128)(2,1)S(1)} %fusion.9), channel_id=1, source_target_pairs={{0,8},{8,16},{16,24},{24,0},{1,9},{9,17},{17,25},{25,1},{2,10},{10... | collective-permute-start | bytes 2752520 | tf_op jit(solution)/shard_map/cond/branch_0_fun/ppermute | solution.py:19
  435.3 113.4 %collective-permute-start.21 = (bf16[448,1024]{1,0:T(8,128)(2,1)S(1)}, bf16[448,1024]{1,0:T(8,128)(2,1)S(1)}, u32[]{:S(2)}, u32[]{:S(2)}) collective-permute-start(bf16[448,1024]{1,0:T(8,128)(2,1)S(1)} %fusion.5), channel_id=1, source_target_pairs={{0,24},{8,0},{16,8},{24,16},{1,25},{9,1},{17,9},{25,17},{2,26},{10... | collective-permute-start | bytes 2752520 | tf_op jit(solution)/shard_map/cond/branch_0_fun/ppermute | solution.py:19
  470.2 83.2 %collective-permute-start.20 = (bf16[448,1024]{1,0:T(8,128)(2,1)S(1)}, bf16[448,1024]{1,0:T(8,128)(2,1)S(1)}, u32[]{:S(2)}, u32[]{:S(2)}) collective-permute-start(bf16[448,1024]{1,0:T(8,128)(2,1)S(1)} %fusion.5), channel_id=1, source_target_pairs={{0,8},{8,16},{16,24},{24,0},{1,9},{9,17},{17,25},{25,1},{2,10},{10... | collective-permute-start | bytes 2752520 | tf_op jit(solution)/shard_map/cond/branch_0_fun/ppermute | solution.py:19
  474.7 113.3 %collective-permute-start.29 = (bf16[448,1024]{1,0:T(8,128)(2,1)S(1)}, bf16[448,1024]{1,0:T(8,128)(2,1)S(1)}, u32[]{:S(2)}, u32[]{:S(2)}) collective-permute-start(bf16[448,1024]{1,0:T(8,128)(2,1)S(1)} %fusion.1), channel_id=1, source_target_pairs={{0,24},{8,0},{16,8},{24,16},{1,25},{9,1},{17,9},{25,17},{2,26},{10... | collective-permute-start | bytes 2752520 | tf_op jit(solution)/shard_map/cond/branch_0_fun/ppermute | solution.py:19
  509.5 83.3 %collective-permute-start.28 = (bf16[448,1024]{1,0:T(8,128)(2,1)S(1)}, bf16[448,1024]{1,0:T(8,128)(2,1)S(1)}, u32[]{:S(2)}, u32[]{:S(2)}) collective-permute-start(bf16[448,1024]{1,0:T(8,128)(2,1)S(1)} %fusion.1), channel_id=1, source_target_pairs={{0,8},{8,16},{16,24},{24,0},{1,9},{9,17},{17,25},{25,1},{2,10},{10... | collective-permute-start | bytes 2752520 | tf_op jit(solution)/shard_map/cond/branch_0_fun/ppermute | solution.py:19
  514.1 113.2 %collective-permute-start.3 = (bf16[448,1024]{1,0:T(8,128)(2,1)S(1)}, bf16[448,1024]{1,0:T(8,128)(2,1)S(1)}, u32[]{:S(2)}, u32[]{:S(2)}) collective-permute-start(bf16[448,1024]{1,0:T(8,128)(2,1)S(1)} %copy-done.12), channel_id=1, source_target_pairs={{0,24},{8,0},{16,8},{24,16},{1,25},{9,1},{17,9},{25,17},{2,26},{10... | collective-permute-start | bytes 2752520 | tf_op jit(solution)/shard_map/cond/branch_0_fun/ppermute | solution.py:19
  548.7 83.4 %collective-permute-start.2 = (bf16[448,1024]{1,0:T(8,128)(2,1)S(1)}, bf16[448,1024]{1,0:T(8,128)(2,1)S(1)}, u32[]{:S(2)}, u32[]{:S(2)}) collective-permute-start(bf16[448,1024]{1,0:T(8,128)(2,1)S(1)} %copy-done.12), channel_id=1, source_target_pairs={{0,8},{8,16},{16,24},{24,0},{1,9},{9,17},{17,25},{25,1},{2,10},{10... | collective-permute-start | bytes 2752520 | tf_op jit(solution)/shard_map/cond/branch_0_fun/ppermute | solution.py:19
  553.4 113.2 %collective-permute-start.11 = (bf16[448,1024]{1,0:T(8,128)(2,1)S(1)}, bf16[448,1024]{1,0:T(8,128)(2,1)S(1)}, u32[]{:S(2)}, u32[]{:S(2)}) collective-permute-start(bf16[448,1024]{1,0:T(8,128)(2,1)S(1)} %copy-done.11), channel_id=1, source_target_pairs={{0,24},{8,0},{16,8},{24,16},{1,25},{9,1},{17,9},{25,17},{2,26},{10... | collective-permute-start | bytes 2752520 | tf_op jit(solution)/shard_map/cond/branch_0_fun/ppermute | solution.py:19
  588.0 83.5 %collective-permute-start.10 = (bf16[448,1024]{1,0:T(8,128)(2,1)S(1)}, bf16[448,1024]{1,0:T(8,128)(2,1)S(1)}, u32[]{:S(2)}, u32[]{:S(2)}) collective-permute-start(bf16[448,1024]{1,0:T(8,128)(2,1)S(1)} %copy-done.11), channel_id=1, source_target_pairs={{0,8},{8,16},{16,24},{24,0},{1,9},{9,17},{17,25},{25,1},{2,10},{10... | collective-permute-start | bytes 2752520 | tf_op jit(solution)/shard_map/cond/branch_0_fun/ppermute | solution.py:19
  592.8 113.1 %collective-permute-start.19 = (bf16[448,1024]{1,0:T(8,128)(2,1)S(1)}, bf16[448,1024]{1,0:T(8,128)(2,1)S(1)}, u32[]{:S(2)}, u32[]{:S(2)}) collective-permute-start(bf16[448,1024]{1,0:T(8,128)(2,1)S(1)} %copy-done.10), channel_id=1, source_target_pairs={{0,24},{8,0},{16,8},{24,16},{1,25},{9,1},{17,9},{25,17},{2,26},{10... | collective-permute-start | bytes 2752520 | tf_op jit(solution)/shard_map/cond/branch_0_fun/ppermute | solution.py:19
  627.3 83.6 %collective-permute-start.18 = (bf16[448,1024]{1,0:T(8,128)(2,1)S(1)}, bf16[448,1024]{1,0:T(8,128)(2,1)S(1)}, u32[]{:S(2)}, u32[]{:S(2)}) collective-permute-start(bf16[448,1024]{1,0:T(8,128)(2,1)S(1)} %copy-done.10), channel_id=1, source_target_pairs={{0,8},{8,16},{16,24},{24,0},{1,9},{9,17},{17,25},{25,1},{2,10},{10... | collective-permute-start | bytes 2752520 | tf_op jit(solution)/shard_map/cond/branch_0_fun/ppermute | solution.py:19
  632.2 97.4 %collective-permute-start.27 = (bf16[448,1024]{1,0:T(8,128)(2,1)S(1)}, bf16[448,1024]{1,0:T(8,128)(2,1)S(1)}, u32[]{:S(2)}, u32[]{:S(2)}) collective-permute-start(bf16[448,1024]{1,0:T(8,128)(2,1)S(1)} %copy-done.9), channel_id=1, source_target_pairs={{0,24},{8,0},{16,8},{24,16},{1,25},{9,1},{17,9},{25,17},{2,26},{10... | collective-permute-start | bytes 2752520 | tf_op jit(solution)/shard_map/cond/branch_0_fun/ppermute | solution.py:19
  (32 other events, 1210.0 us)
Sparse Core Ops, SparseCore 0:
  19.9 44.6 all-gather.8
  66.5 40.0 all-gather.14
  108.5 30.3 all-gather.10
  140.6 27.8 all-gather.12

commit v3 on v2

v3 whole, which is shorter than its diff:
```python
import jax
import jax.numpy as jnp
from jax import lax
from jax.sharding import PartitionSpec as P

base_rate = 40.0
moment_decay = 0.9
keep_share = 0.5
back_share = 0.3
front_share = 0.2
tokens_axis = (((0,), (0,)), ((), ()))
col_blocks = 4


def shifted(value, axis, steps):
    count = lax.axis_size(axis)
    pairs = [(source, (source + steps) % count) for source in range(count)]
    return lax.ppermute(value, axis, pairs)


def block_count(length, target, quantum):
    for count in range(target, 0, -1):
        if length % count == 0 and (length // count) % quantum == 0:
            return count
    return 1


def row_sizes(rows, quantum=16):
    first = 128 if rows >= 512 and rows % quantum == 0 else rows
    rest = rows - first
    if rest == 0:
        return [first]
    units = rest // quantum
    parts = [units // 3 + (1 if i < units % 3 else 0) for i in range(3)]
    return [first] + [p * quantum for p in parts if p > 0]


def pipeline(amount, groups, params, momentum, hidden, cotangent, push_weight, rate, direct):
    nodes = lax.axis_size("node")
    rows_total = params.shape[1]
    acts = hidden.reshape(hidden.shape[0], nodes, rows_total)
    width = cotangent.shape[1]
    n_cols = block_count(width, col_blocks, 128)
    col_size = width // n_cols
    paired = (2 * amount) % groups == 0
    w_minus = jnp.where(direct, back_share, front_share).astype(jnp.float32)
    w_plus = jnp.where(direct, front_share, back_share).astype(jnp.float32)
    cots = [
        lax.all_gather(cotangent[:, b * col_size:(b + 1) * col_size], "node", axis=0, tiled=True)
        for b in range(n_cols)
    ]
    mixed = jnp.zeros(params.shape[1:], jnp.bfloat16)
    start = 0
    last = None
    for size in row_sizes(rows_total):
        piece = acts[:, :, start:start + size]
        if last is not None:
            piece, last = lax.optimization_barrier((piece, last))
        cols = lax.all_to_all(piece, "node", split_axis=1, concat_axis=0, tiled=True)
        cols = cols.reshape(-1, size)
        tok_group = cols.shape[0]
        rows = slice(start, start + size)
        for b in range(n_cols):
            span = slice(b * col_size, (b + 1) * col_size)
            grad = lax.dot_general(cols, cots[b], tokens_axis, preferred_element_type=jnp.float32)
            grad = grad / tok_group
            renewed = moment_decay * momentum[0, rows, span].astype(jnp.float32) + grad
            half = (params[0, rows, span].astype(jnp.float32) - rate * renewed).astype(jnp.bfloat16)
            if b == 0:
                last = half
            minus = shifted(half, "grp", amount)
            if paired:
                peers = (back_share * minus.astype(jnp.float32)) + front_share * minus.astype(jnp.float32)
            else:
                plus = shifted(half, "grp", groups - amount)
                peers = w_minus * minus.astype(jnp.float32) + w_plus * plus.astype(jnp.float32)
            total = keep_share * half.astype(jnp.float32) + peers
            mixed = lax.dynamic_update_slice(mixed, total.astype(jnp.bfloat16), (start, b * col_size))
        start += size
    weight_minus = shifted(push_weight, "grp", amount)
    weight_plus = shifted(push_weight, "grp", groups - amount)
    new_weight = keep_share * push_weight + w_minus * weight_minus + w_plus * weight_plus
    return mixed[None], new_weight


def per_device(params, momentum, hidden, cotangent, push_weight, offsets, step):
    groups = lax.axis_size("grp")
    position = step[0]
    offset = offsets[position]
    rate = base_rate * (1.0 - 0.5 * position.astype(jnp.float32) / offsets.shape[0])
    amounts = list(range(1, groups // 2 + 1))
    direct = offset <= groups // 2
    index = jnp.where(direct, offset, groups - offset) - 1
    branches = [
        (lambda *a, amount=amount: pipeline(amount, groups, *a))
        for amount in amounts
    ]
    return lax.switch(
        index, branches, params, momentum, hidden[0], cotangent[0], push_weight, rate, direct
    )


def solution(mesh):
    in_specs = (
        P("grp", "node", None),
        P("grp", "node", None),
        P("grp", "node", None),
        P("grp", "node", None),
        P("grp"),
        P(),
        P(),
    )
    out_specs = (P("grp", "node", None), P("grp"))
    return jax.shard_map(
        per_device, mesh=mesh, in_specs=in_specs, out_specs=out_specs, check_vma=False
    )
```

time: 891 us -> 789 us (0.89)
  starting transfers between devices: 75.4 us -> 303 us
  waiting for transfers between devices: 503 us -> 321 us
  other arithmetic: 142 us -> 37.5 us
  blocking collectives: 62.4 us -> 0 us
  local copies, waits for them, and re-layouts: 16.8 us -> 27 us
    ppermute x34, waiting for transfers between devices: 477 us -> 233 us  [shifted(): return lax.ppermute(value, axis, pairs)]
    ppermute x34, starting transfers between devices: 71.7 us -> 288 us  [shifted(): return lax.ppermute(value, axis, pairs)]
    broadcast_in_dim x1 -> x0, other arithmetic: 119 us -> none  [pipeline(): return (mixed[None], new_weight)]
    all_to_all x3 -> x0, blocking collectives: 62.4 us -> none  [pipeline(): lax.all_to_all(acts[:, :, a, :], 'node', split_axis=1, concat_axis=0, til...]
    all_gather x4, waiting for transfers between devices: 18.5 us -> 78.6 us  [pipeline(): lax.all_gather(cotangent[:, b * col_size:(b + 1) * col_size], 'node', axi...]
    dynamic_update_slice x0 -> x15, other arithmetic: none -> 37.3 us  [pipeline(): lax.dynamic_update_slice(mixed, total.astype(jnp.bfloat16), (start, b * c...]
    convert_element_type x16 -> x1, other arithmetic: 23.4 us -> 0.15 us  [pipeline(): total.astype(jnp.bfloat16)]
    all_to_all x1 -> x4, starting transfers between devices: 3.55 us -> 14.6 us  [pipeline(): lax.all_to_all(piece, 'node', split_axis=1, concat_axis=0, tiled=True)]
  transfers between devices with their start and end apart: 39 -> 42, of which waited for: 31 -> 20; matrix products, arithmetic and copies ran while one was open for 9% -> 14% of each run, Pallas kernels for 0% -> 0%
where the time goes in v3:
time: 789 us; the launch traced here: 780 us
  waiting for transfers between devices  321 us (41%)
  starting transfers between devices  303 us (38%)
  matrix products  58.8 us (7%)
  other arithmetic  37.5 us (5%)
  local copies, waits for them, and re-layouts  27 us (3%)
  between operations  17.9 us (2%)
  loops' own time  14.8 us (2%)
    ppermute x34, starting transfers between devices, shifted(): return lax.ppermute(value, axis, pairs)  288 us
    ppermute x34, waiting for transfers between devices, shifted(): return lax.ppermute(value, axis, pairs)  233 us
    all_gather x4, waiting for transfers between devices, pipeline(): lax.all_gather(cotangent[:, b * col_size:(b + 1) * col_size], 'node', axi...  78.6 us
    dot_general x16, matrix products, pipeline(): lax.dot_general(cols, cots[b], tokens_axis, preferred_element_type=jnp.fl...  58.8 us
    dynamic_update_slice x15, other arithmetic, pipeline(): lax.dynamic_update_slice(mixed, total.astype(jnp.bfloat16), (start, b * c...  37.3 us
  transfers between devices with their start and end apart: 42, of which 20 were waited for; matrix products, arithmetic and copies ran while one was open for 14% of the time, Pallas kernels for 0%

profile of v3, /device:TPU:0, one launch (start us, length us, event | category | flops | bytes accessed | tf_op | source)
XLA Modules:
  0.0 779.8 jit_solution(13030687299762644359)
XLA Ops:
  11.0 760.7 %conditional.1 = (bf16[1,1792,4096]{2,1,0:T(8,128)(2,1)}, f32[1]{0:T(128)}) conditional(s32[]{:T(128)} %clamp.3, (bf16[1,1792,4096]{2,1,0:T(8,128)(2,1)}, f32[]{:T(128)}, bf16[1,1792,4096]{2,1,0:T(8,128)(2,1)}, bf16[1,128,14336]{2,1,0:T(8,128)(2,1)}, bf16[128,4096]{1,0:T(8,128)(2,1)}, /*index=5*/pred[]{:T(512)}, f32[1]{0:T(128)}) %tuple.55, ...), branch_computations={%region_0.1_spmd, %region_1.2_spmd} | conditional | flops 15157166080 | bytes 441467904 | solution.py:98
  51.6 22.6 %all-gather.11.cloned.1.call-done = bf16[1024,1024]{1,0:T(8,128)(2,1)} async-done(((bf16[128,1024]{1,0:T(8,128)(2,1)}), bf16[1024,1024]{1,0:T(8,128)(2,1)}) %all-gather.11.cloned.1.call-update) | async-done | bytes 2097168 | tf_op jit(solution)/shard_map/cond/branch_0_fun/all_gather | solution.py:49
  80.3 23.7 %all-gather.13.cloned.1.call-done = bf16[1024,1024]{1,0:T(8,128)(2,1)} async-done(((bf16[128,1024]{1,0:T(8,128)(2,1)}), bf16[1024,1024]{1,0:T(8,128)(2,1)}) %all-gather.13.cloned.1.call-update) | async-done | bytes 2097168 | tf_op jit(solution)/shard_map/cond/branch_0_fun/all_gather | solution.py:49
  111.3 27.5 %all-gather.15.cloned.1.call-done = bf16[1024,1024]{1,0:T(8,128)(2,1)} async-done(((bf16[128,1024]{1,0:T(8,128)(2,1)}), bf16[1024,1024]{1,0:T(8,128)(2,1)}) %all-gather.15.cloned.1.call-update) | async-done | bytes 2097168 | tf_op jit(solution)/shard_map/cond/branch_0_fun/all_gather | solution.py:49
  226.5 21.9 %collective-permute-start.14 = (bf16[560,1024]{1,0:T(8,128)(2,1)S(1)}, bf16[560,1024]{1,0:T(8,128)(2,1)S(1)}, u32[]{:S(2)}, u32[]{:S(2)}) collective-permute-start(bf16[560,1024]{1,0:T(8,128)(2,1)S(1)} %copy-done.17), channel_id=1, source_target_pairs={{0,8},{8,16},{16,24},{24,0},{1,9},{9,17},{17,25},{25,1},{2,10},{10... | collective-permute-start | bytes 3440648 | tf_op jit(solution)/shard_map/cond/branch_0_fun/ppermute | solution.py:18
  249.7 26.0 %collective-permute-start.15 = (bf16[560,1024]{1,0:T(8,128)(2,1)S(1)}, bf16[560,1024]{1,0:T(8,128)(2,1)S(1)}, u32[]{:S(2)}, u32[]{:S(2)}) collective-permute-start(bf16[560,1024]{1,0:T(8,128)(2,1)S(1)} %copy-done.17), channel_id=1, source_target_pairs={{0,24},{8,0},{16,8},{24,16},{1,25},{9,1},{17,9},{25,17},{2,26},{10... | collective-permute-start | bytes 3440648 | tf_op jit(solution)/shard_map/cond/branch_0_fun/ppermute | solution.py:18
  298.9 26.0 %collective-permute-start.17 = (bf16[560,1024]{1,0:T(8,128)(2,1)}, bf16[560,1024]{1,0:T(8,128)(2,1)}, u32[]{:S(2)}, u32[]{:S(2)}) collective-permute-start(bf16[560,1024]{1,0:T(8,128)(2,1)} %fusion.3), channel_id=1, source_target_pairs={{0,24},{8,0},{16,8},{24,16},{1,25},{9,1},{17,9},{25,17},{2,26},{10... | collective-permute-start | bytes 3440648 | tf_op jit(solution)/shard_map/cond/branch_0_fun/ppermute | solution.py:18
  328.3 19.7 %collective-permute-done.14 = bf16[560,1024]{1,0:T(8,128)(2,1)S(1)} collective-permute-done((bf16[560,1024]{1,0:T(8,128)(2,1)S(1)}, bf16[560,1024]{1,0:T(8,128)(2,1)S(1)}, u32[]{:S(2)}, u32[]{:S(2)}) %collective-permute-start.14) | collective-permute-done | bytes 1146912 | tf_op jit(solution)/shard_map/cond/branch_0_fun/ppermute | solution.py:18
  348.0 25.9 %collective-permute-start.19 = (bf16[560,1024]{1,0:T(8,128)(2,1)}, bf16[560,1024]{1,0:T(8,128)(2,1)}, u32[]{:S(2)}, u32[]{:S(2)}) collective-permute-start(bf16[560,1024]{1,0:T(8,128)(2,1)} %fusion.2), channel_id=1, source_target_pairs={{0,24},{8,0},{16,8},{24,16},{1,25},{9,1},{17,9},{25,17},{2,26},{10... | collective-permute-start | bytes 3440648 | tf_op jit(solution)/shard_map/cond/branch_0_fun/ppermute | solution.py:18
  376.2 21.1 %collective-permute-done.16 = bf16[560,1024]{1,0:T(8,128)(2,1)} collective-permute-done((bf16[560,1024]{1,0:T(8,128)(2,1)}, bf16[560,1024]{1,0:T(8,128)(2,1)}, u32[]{:S(2)}, u32[]{:S(2)}) %collective-permute-start.16) | collective-permute-done | bytes 1146912 | tf_op jit(solution)/shard_map/cond/branch_0_fun/ppermute | solution.py:18
  397.3 26.3 %collective-permute-start.21 = (bf16[560,1024]{1,0:T(8,128)(2,1)}, bf16[560,1024]{1,0:T(8,128)(2,1)S(1)}, u32[]{:S(2)}, u32[]{:S(2)}) collective-permute-start(bf16[560,1024]{1,0:T(8,128)(2,1)} %fusion.1), channel_id=1, source_target_pairs={{0,24},{8,0},{16,8},{24,16},{1,25},{9,1},{17,9},{25,17},{2,26},{10... | collective-permute-start | bytes 3440648 | tf_op jit(solution)/shard_map/cond/branch_0_fun/ppermute | solution.py:18
  446.5 25.8 %collective-permute-start.23 = (bf16[560,1024]{1,0:T(8,128)(2,1)S(1)}, bf16[560,1024]{1,0:T(8,128)(2,1)S(1)}, u32[]{:S(2)}, u32[]{:S(2)}) collective-permute-start(bf16[560,1024]{1,0:T(8,128)(2,1)S(1)} %copy-done.16), channel_id=1, source_target_pairs={{0,24},{8,0},{16,8},{24,16},{1,25},{9,1},{17,9},{25,17},{2,26},{10... | collective-permute-start | bytes 3440648 | tf_op jit(solution)/shard_map/cond/branch_0_fun/ppermute | solution.py:18
  472.3 23.4 %collective-permute-done.20 = bf16[560,1024]{1,0:T(8,128)(2,1)} collective-permute-done((bf16[560,1024]{1,0:T(8,128)(2,1)}, bf16[560,1024]{1,0:T(8,128)(2,1)}, u32[]{:S(2)}, u32[]{:S(2)}) %collective-permute-start.20) | collective-permute-done | bytes 1146912 | tf_op jit(solution)/shard_map/cond/branch_0_fun/ppermute | solution.py:18
  495.7 25.8 %collective-permute-start.25 = (bf16[544,1024]{1,0:T(8,128)(2,1)S(1)}, bf16[544,1024]{1,0:T(8,128)(2,1)S(1)}, u32[]{:S(2)}, u32[]{:S(2)}) collective-permute-start(bf16[544,1024]{1,0:T(8,128)(2,1)S(1)} %fusion.19), channel_id=1, source_target_pairs={{0,24},{8,0},{16,8},{24,16},{1,25},{9,1},{17,9},{25,17},{2,26},{10... | collective-permute-start | bytes 3342344 | tf_op jit(solution)/shard_map/cond/branch_0_fun/ppermute | solution.py:18
  528.3 16.4 %collective-permute-done.22 = bf16[560,1024]{1,0:T(8,128)(2,1)S(1)} collective-permute-done((bf16[560,1024]{1,0:T(8,128)(2,1)S(1)}, bf16[560,1024]{1,0:T(8,128)(2,1)S(1)}, u32[]{:S(2)}, u32[]{:S(2)}) %collective-permute-start.22) | collective-permute-done | bytes 1146912 | tf_op jit(solution)/shard_map/cond/branch_0_fun/ppermute | solution.py:18
  544.8 25.8 %collective-permute-start.27 = (bf16[544,1024]{1,0:T(8,128)(2,1)S(1)}, bf16[544,1024]{1,0:T(8,128)(2,1)S(1)}, u32[]{:S(2)}, u32[]{:S(2)}) collective-permute-start(bf16[544,1024]{1,0:T(8,128)(2,1)S(1)} %fusion.18), channel_id=1, source_target_pairs={{0,24},{8,0},{16,8},{24,16},{1,25},{9,1},{17,9},{25,17},{2,26},{10... | collective-permute-start | bytes 3342344 | tf_op jit(solution)/shard_map/cond/branch_0_fun/ppermute | solution.py:18
  574.2 19.0 %collective-permute-done.24 = bf16[544,1024]{1,0:T(8,128)(2,1)S(1)} collective-permute-done((bf16[544,1024]{1,0:T(8,128)(2,1)S(1)}, bf16[544,1024]{1,0:T(8,128)(2,1)S(1)}, u32[]{:S(2)}, u32[]{:S(2)}) %collective-permute-start.24) | collective-permute-done | bytes 1114144 | tf_op jit(solution)/shard_map/cond/branch_0_fun/ppermute | solution.py:18
  593.2 25.0 %collective-permute-start.29 = (bf16[544,1024]{1,0:T(8,128)(2,1)S(1)}, bf16[544,1024]{1,0:T(8,128)(2,1)S(1)}, u32[]{:S(2)}, u32[]{:S(2)}) collective-permute-start(bf16[544,1024]{1,0:T(8,128)(2,1)S(1)} %fusion.17), channel_id=1, source_target_pairs={{0,24},{8,0},{16,8},{24,16},{1,25},{9,1},{17,9},{25,17},{2,26},{10... | collective-permute-start | bytes 3342344 | tf_op jit(solution)/shard_map/cond/branch_0_fun/ppermute | solution.py:18
  621.7 19.4 %collective-permute-done.26 = bf16[544,1024]{1,0:T(8,128)(2,1)S(1)} collective-permute-done((bf16[544,1024]{1,0:T(8,128)(2,1)S(1)}, bf16[544,1024]{1,0:T(8,128)(2,1)S(1)}, u32[]{:S(2)}, u32[]{:S(2)}) %collective-permute-start.26) | collective-permute-done | bytes 1114144 | tf_op jit(solution)/shard_map/cond/branch_0_fun/ppermute | solution.py:18
  641.0 25.0 %collective-permute-start.31 = (bf16[544,1024]{1,0:T(8,128)(2,1)S(1)}, bf16[544,1024]{1,0:T(8,128)(2,1)S(1)}, u32[]{:S(2)}, u32[]{:S(2)}) collective-permute-start(bf16[544,1024]{1,0:T(8,128)(2,1)S(1)} %fusion.16), channel_id=1, source_target_pairs={{0,24},{8,0},{16,8},{24,16},{1,25},{9,1},{17,9},{25,17},{2,26},{10... | collective-permute-start | bytes 3342344 | tf_op jit(solution)/shard_map/cond/branch_0_fun/ppermute | solution.py:18
  671.4 17.4 %collective-permute-done.28 = bf16[544,1024]{1,0:T(8,128)(2,1)S(1)} collective-permute-done((bf16[544,1024]{1,0:T(8,128)(2,1)S(1)}, bf16[544,1024]{1,0:T(8,128)(2,1)S(1)}, u32[]{:S(2)}, u32[]{:S(2)}) %collective-permute-start.28) | collective-permute-done | bytes 1114144 | tf_op jit(solution)/shard_map/cond/branch_0_fun/ppermute | solution.py:18
  688.8 22.3 %collective-permute-done.29 = bf16[544,1024]{1,0:T(8,128)(2,1)S(1)} collective-permute-done((bf16[544,1024]{1,0:T(8,128)(2,1)S(1)}, bf16[544,1024]{1,0:T(8,128)(2,1)S(1)}, u32[]{:S(2)}, u32[]{:S(2)}) %collective-permute-start.29) | collective-permute-done | bytes 1114144 | tf_op jit(solution)/shard_map/cond/branch_0_fun/ppermute | solution.py:18
  712.9 23.7 %collective-permute-done.30 = bf16[544,1024]{1,0:T(8,128)(2,1)S(1)} collective-permute-done((bf16[544,1024]{1,0:T(8,128)(2,1)S(1)}, bf16[544,1024]{1,0:T(8,128)(2,1)S(1)}, u32[]{:S(2)}, u32[]{:S(2)}) %collective-permute-start.30) | collective-permute-done | bytes 1114144 | tf_op jit(solution)/shard_map/cond/branch_0_fun/ppermute | solution.py:18
  736.6 20.8 %collective-permute-done.31 = bf16[544,1024]{1,0:T(8,128)(2,1)S(1)} collective-permute-done((bf16[544,1024]{1,0:T(8,128)(2,1)S(1)}, bf16[544,1024]{1,0:T(8,128)(2,1)S(1)}, u32[]{:S(2)}, u32[]{:S(2)}) %collective-permute-start.31) | collective-permute-done | bytes 1114144 | tf_op jit(solution)/shard_map/cond/branch_0_fun/ppermute | solution.py:18
  (136 shorter events, 216.5 us)
Async XLA Ops:
  14.8 123.9 %all-gather.15.cloned.1.call-start = ((), (), s32[]{:S(2)}) async-start(), calls=%async_computation.11 | async-start | bytes 2359296 | tf_op jit(solution)/shard_map/cond/branch_0_fun/all_gather | solution.py:49
  48.4 96.6 %collective-permute-start.1 = (bf16[128,1024]{1,0:T(8,128)(2,1)S(1)}, bf16[128,1024]{1,0:T(8,128)(2,1)S(1)}, u32[]{:S(2)}, u32[]{:S(2)}) collective-permute-start(bf16[128,1024]{1,0:T(8,128)(2,1)S(1)} %fusion.36), channel_id=1, source_target_pairs={{0,24},{8,0},{16,8},{24,16},{1,25},{9,1},{17,9},{25,17},{2,26},{10... | collective-permute-start | bytes 786440 | tf_op jit(solution)/shard_map/cond/branch_0_fun/ppermute | solution.py:18
  178.2 101.6 %collective-permute-start.11 = (bf16[560,1024]{1,0:T(8,128)(2,1)}, bf16[560,1024]{1,0:T(8,128)(2,1)}, u32[]{:S(2)}, u32[]{:S(2)}) collective-permute-start(bf16[560,1024]{1,0:T(8,128)(2,1)} %fusion.6), channel_id=1, source_target_pairs={{0,24},{8,0},{16,8},{24,16},{1,25},{9,1},{17,9},{25,17},{2,26},{10... | collective-permute-start | bytes 3440648 | tf_op jit(solution)/shard_map/cond/branch_0_fun/ppermute | solution.py:18
  191.0 107.9 %collective-permute-start.12 = (bf16[560,1024]{1,0:T(8,128)(2,1)}, bf16[560,1024]{1,0:T(8,128)(2,1)}, u32[]{:S(2)}, u32[]{:S(2)}) collective-permute-start(bf16[560,1024]{1,0:T(8,128)(2,1)} %fusion.5), channel_id=1, source_target_pairs={{0,8},{8,16},{16,24},{24,0},{1,9},{9,17},{17,25},{25,1},{2,10},{10... | collective-permute-start | bytes 3440648 | tf_op jit(solution)/shard_map/cond/branch_0_fun/ppermute | solution.py:18
  208.2 167.5 %all-to-all-start.3 = ((bf16[128,8,544]{0,2,1:T(8,128)(2,1)}), bf16[128,8,544]{0,2,1:T(8,128)(2,1)S(1)}, u32[]{:S(2)}, u32[]{:S(2)}) async-start(bf16[128,8,544]{0,2,1:T(8,128)(2,1)} %slice.243), calls=%async_computation.3 | async-start | bytes 2228224 | tf_op jit(solution)/shard_map/cond/branch_0_fun/all_to_all | solution.py:59
  221.5 103.3 %collective-permute-start.13 = (bf16[560,1024]{1,0:T(8,128)(2,1)}, bf16[560,1024]{1,0:T(8,128)(2,1)S(1)}, u32[]{:S(2)}, u32[]{:S(2)}) collective-permute-start(bf16[560,1024]{1,0:T(8,128)(2,1)} %fusion.5), channel_id=1, source_target_pairs={{0,24},{8,0},{16,8},{24,16},{1,25},{9,1},{17,9},{25,17},{2,26},{10... | collective-permute-start | bytes 3440648 | tf_op jit(solution)/shard_map/cond/branch_0_fun/ppermute | solution.py:18
  226.5 121.4 %collective-permute-start.14 = (bf16[560,1024]{1,0:T(8,128)(2,1)S(1)}, bf16[560,1024]{1,0:T(8,128)(2,1)S(1)}, u32[]{:S(2)}, u32[]{:S(2)}) collective-permute-start(bf16[560,1024]{1,0:T(8,128)(2,1)S(1)} %copy-done.17), channel_id=1, source_target_pairs={{0,8},{8,16},{16,24},{24,0},{1,9},{9,17},{17,25},{25,1},{2,10},{10... | collective-permute-start | bytes 3440648 | tf_op jit(solution)/shard_map/cond/branch_0_fun/ppermute | solution.py:18
  249.7 124.2 %collective-permute-start.15 = (bf16[560,1024]{1,0:T(8,128)(2,1)S(1)}, bf16[560,1024]{1,0:T(8,128)(2,1)S(1)}, u32[]{:S(2)}, u32[]{:S(2)}) collective-permute-start(bf16[560,1024]{1,0:T(8,128)(2,1)S(1)} %copy-done.17), channel_id=1, source_target_pairs={{0,24},{8,0},{16,8},{24,16},{1,25},{9,1},{17,9},{25,17},{2,26},{10... | collective-permute-start | bytes 3440648 | tf_op jit(solution)/shard_map/cond/branch_0_fun/ppermute | solution.py:18
  279.9 117.4 %collective-permute-start.16 = (bf16[560,1024]{1,0:T(8,128)(2,1)}, bf16[560,1024]{1,0:T(8,128)(2,1)}, u32[]{:S(2)}, u32[]{:S(2)}) collective-permute-start(bf16[560,1024]{1,0:T(8,128)(2,1)} %fusion.3), channel_id=1, source_target_pairs={{0,8},{8,16},{16,24},{24,0},{1,9},{9,17},{17,25},{25,1},{2,10},{10... | collective-permute-start | bytes 3440648 | tf_op jit(solution)/shard_map/cond/branch_0_fun/ppermute | solution.py:18
  298.9 131.3 %collective-permute-start.17 = (bf16[560,1024]{1,0:T(8,128)(2,1)}, bf16[560,1024]{1,0:T(8,128)(2,1)}, u32[]{:S(2)}, u32[]{:S(2)}) collective-permute-start(bf16[560,1024]{1,0:T(8,128)(2,1)} %fusion.3), channel_id=1, source_target_pairs={{0,24},{8,0},{16,8},{24,16},{1,25},{9,1},{17,9},{25,17},{2,26},{10... | collective-permute-start | bytes 3440648 | tf_op jit(solution)/shard_map/cond/branch_0_fun/ppermute | solution.py:18
  324.8 121.6 %collective-permute-start.18 = (bf16[560,1024]{1,0:T(8,128)(2,1)}, bf16[560,1024]{1,0:T(8,128)(2,1)}, u32[]{:S(2)}, u32[]{:S(2)}) collective-permute-start(bf16[560,1024]{1,0:T(8,128)(2,1)} %fusion.2), channel_id=1, source_target_pairs={{0,8},{8,16},{16,24},{24,0},{1,9},{9,17},{17,25},{25,1},{2,10},{10... | collective-permute-start | bytes 3440648 | tf_op jit(solution)/shard_map/cond/branch_0_fun/ppermute | solution.py:18
  348.0 124.3 %collective-permute-start.19 = (bf16[560,1024]{1,0:T(8,128)(2,1)}, bf16[560,1024]{1,0:T(8,128)(2,1)}, u32[]{:S(2)}, u32[]{:S(2)}) collective-permute-start(bf16[560,1024]{1,0:T(8,128)(2,1)} %fusion.2), channel_id=1, source_target_pairs={{0,24},{8,0},{16,8},{24,16},{1,25},{9,1},{17,9},{25,17},{2,26},{10... | collective-permute-start | bytes 3440648 | tf_op jit(solution)/shard_map/cond/branch_0_fun/ppermute | solution.py:18
  373.9 121.8 %collective-permute-start.20 = (bf16[560,1024]{1,0:T(8,128)(2,1)}, bf16[560,1024]{1,0:T(8,128)(2,1)}, u32[]{:S(2)}, u32[]{:S(2)}) collective-permute-start(bf16[560,1024]{1,0:T(8,128)(2,1)} %fusion.1), channel_id=1, source_target_pairs={{0,8},{8,16},{16,24},{24,0},{1,9},{9,17},{17,25},{25,1},{2,10},{10... | collective-permute-start | bytes 3440648 | tf_op jit(solution)/shard_map/cond/branch_0_fun/ppermute | solution.py:18
  397.3 124.2 %collective-permute-start.21 = (bf16[560,1024]{1,0:T(8,128)(2,1)}, bf16[560,1024]{1,0:T(8,128)(2,1)S(1)}, u32[]{:S(2)}, u32[]{:S(2)}) collective-permute-start(bf16[560,1024]{1,0:T(8,128)(2,1)} %fusion.1), channel_id=1, source_target_pairs={{0,24},{8,0},{16,8},{24,16},{1,25},{9,1},{17,9},{25,17},{2,26},{10... | collective-permute-start | bytes 3440648 | tf_op jit(solution)/shard_map/cond/branch_0_fun/ppermute | solution.py:18
  430.2 114.6 %collective-permute-start.22 = (bf16[560,1024]{1,0:T(8,128)(2,1)S(1)}, bf16[560,1024]{1,0:T(8,128)(2,1)S(1)}, u32[]{:S(2)}, u32[]{:S(2)}) collective-permute-start(bf16[560,1024]{1,0:T(8,128)(2,1)S(1)} %copy-done.16), channel_id=1, source_target_pairs={{0,8},{8,16},{16,24},{24,0},{1,9},{9,17},{17,25},{25,1},{2,10},{10... | collective-permute-start | bytes 3440648 | tf_op jit(solution)/shard_map/cond/branch_0_fun/ppermute | solution.py:18
  446.5 127.8 %collective-permute-start.23 = (bf16[560,1024]{1,0:T(8,128)(2,1)S(1)}, bf16[560,1024]{1,0:T(8,128)(2,1)S(1)}, u32[]{:S(2)}, u32[]{:S(2)}) collective-permute-start(bf16[560,1024]{1,0:T(8,128)(2,1)S(1)} %copy-done.16), channel_id=1, source_target_pairs={{0,24},{8,0},{16,8},{24,16},{1,25},{9,1},{17,9},{25,17},{2,26},{10... | collective-permute-start | bytes 3440648 | tf_op jit(solution)/shard_map/cond/branch_0_fun/ppermute | solution.py:18
  472.3 120.9 %collective-permute-start.24 = (bf16[544,1024]{1,0:T(8,128)(2,1)S(1)}, bf16[544,1024]{1,0:T(8,128)(2,1)S(1)}, u32[]{:S(2)}, u32[]{:S(2)}) collective-permute-start(bf16[544,1024]{1,0:T(8,128)(2,1)S(1)} %fusion.19), channel_id=1, source_target_pairs={{0,8},{8,16},{16,24},{24,0},{1,9},{9,17},{17,25},{25,1},{2,10},{10... | collective-permute-start | bytes 3342344 | tf_op jit(solution)/shard_map/cond/branch_0_fun/ppermute | solution.py:18
  495.7 126.0 %collective-permute-start.25 = (bf16[544,1024]{1,0:T(8,128)(2,1)S(1)}, bf16[544,1024]{1,0:T(8,128)(2,1)S(1)}, u32[]{:S(2)}, u32[]{:S(2)}) collective-permute-start(bf16[544,1024]{1,0:T(8,128)(2,1)S(1)} %fusion.19), channel_id=1, source_target_pairs={{0,24},{8,0},{16,8},{24,16},{1,25},{9,1},{17,9},{25,17},{2,26},{10... | collective-permute-start | bytes 3342344 | tf_op jit(solution)/shard_map/cond/branch_0_fun/ppermute | solution.py:18
  521.5 119.6 %collective-permute-start.26 = (bf16[544,1024]{1,0:T(8,128)(2,1)S(1)}, bf16[544,1024]{1,0:T(8,128)(2,1)S(1)}, u32[]{:S(2)}, u32[]{:S(2)}) collective-permute-start(bf16[544,1024]{1,0:T(8,128)(2,1)S(1)} %fusion.18), channel_id=1, source_target_pairs={{0,8},{8,16},{16,24},{24,0},{1,9},{9,17},{17,25},{25,1},{2,10},{10... | collective-permute-start | bytes 3342344 | tf_op jit(solution)/shard_map/cond/branch_0_fun/ppermute | solution.py:18
  544.8 124.9 %collective-permute-start.27 = (bf16[544,1024]{1,0:T(8,128)(2,1)S(1)}, bf16[544,1024]{1,0:T(8,128)(2,1)S(1)}, u32[]{:S(2)}, u32[]{:S(2)}) collective-permute-start(bf16[544,1024]{1,0:T(8,128)(2,1)S(1)} %fusion.18), channel_id=1, source_target_pairs={{0,24},{8,0},{16,8},{24,16},{1,25},{9,1},{17,9},{25,17},{2,26},{10... | collective-permute-start | bytes 3342344 | tf_op jit(solution)/shard_map/cond/branch_0_fun/ppermute | solution.py:18
  574.2 114.6 %collective-permute-start.28 = (bf16[544,1024]{1,0:T(8,128)(2,1)S(1)}, bf16[544,1024]{1,0:T(8,128)(2,1)S(1)}, u32[]{:S(2)}, u32[]{:S(2)}) collective-permute-start(bf16[544,1024]{1,0:T(8,128)(2,1)S(1)} %fusion.17), channel_id=1, source_target_pairs={{0,8},{8,16},{16,24},{24,0},{1,9},{9,17},{17,25},{25,1},{2,10},{10... | collective-permute-start | bytes 3342344 | tf_op jit(solution)/shard_map/cond/branch_0_fun/ppermute | solution.py:18
  593.2 117.9 %collective-permute-start.29 = (bf16[544,1024]{1,0:T(8,128)(2,1)S(1)}, bf16[544,1024]{1,0:T(8,128)(2,1)S(1)}, u32[]{:S(2)}, u32[]{:S(2)}) collective-permute-start(bf16[544,1024]{1,0:T(8,128)(2,1)S(1)} %fusion.17), channel_id=1, source_target_pairs={{0,24},{8,0},{16,8},{24,16},{1,25},{9,1},{17,9},{25,17},{2,26},{10... | collective-permute-start | bytes 3342344 | tf_op jit(solution)/shard_map/cond/branch_0_fun/ppermute | solution.py:18
  621.7 115.0 %collective-permute-start.30 = (bf16[544,1024]{1,0:T(8,128)(2,1)S(1)}, bf16[544,1024]{1,0:T(8,128)(2,1)S(1)}, u32[]{:S(2)}, u32[]{:S(2)}) collective-permute-start(bf16[544,1024]{1,0:T(8,128)(2,1)S(1)} %fusion.16), channel_id=1, source_target_pairs={{0,8},{8,16},{16,24},{24,0},{1,9},{9,17},{17,25},{25,1},{2,10},{10... | collective-permute-start | bytes 3342344 | tf_op jit(solution)/shard_map/cond/branch_0_fun/ppermute | solution.py:18
  641.0 116.4 %collective-permute-start.31 = (bf16[544,1024]{1,0:T(8,128)(2,1)S(1)}, bf16[544,1024]{1,0:T(8,128)(2,1)S(1)}, u32[]{:S(2)}, u32[]{:S(2)}) collective-permute-start(bf16[544,1024]{1,0:T(8,128)(2,1)S(1)} %fusion.16), channel_id=1, source_target_pairs={{0,24},{8,0},{16,8},{24,16},{1,25},{9,1},{17,9},{25,17},{2,26},{10... | collective-permute-start | bytes 3342344 | tf_op jit(solution)/shard_map/cond/branch_0_fun/ppermute | solution.py:18
  (32 other events, 954.4 us)
Sparse Core Ops, SparseCore 0:
  13.8 31.6 all-gather.8
  47.4 26.7 all-gather.10
  76.1 27.8 all-gather.12
  105.8 32.9 all-gather.14
